TPU v7x, 32 devices: a whole 2x2x4 slice. The times are simulated.
32 devices in a mesh: parts: 2 (over x), seq: 16 (over z, y, core).
Axes of the slice: x: 2, y: 2, z: 4, core: 2. Of those that a mesh axis runs over, the one named last changes fastest.
Arguments:
- queries: bfloat16 [8192, 4096], P(('parts', 'seq')), parts along dimension 0, may hold values from -6 to 6
- keys: bfloat16 [8192, 256], P(('parts', 'seq')), parts along dimension 0, may hold values from -6 to 6
- values: bfloat16 [8192, 256], P(('parts', 'seq')), parts along dimension 0, may hold values from -6 to 6
- outputs: bfloat16 [8192, 4096], P(('parts', 'seq')), parts along dimension 0, may hold values from -0.59765625 to 0.59765625
- out_grad: bfloat16 [8192, 4096], P(('parts', 'seq')), parts along dimension 0, may hold values from -6 to 6
- logsumexp: float32 [32, 8192], P(None, ('parts', 'seq')), parts along dimension 1, may hold values from 4 to 7
- doc_lengths: int32 [32], P('parts'), parts along dimension 0, may hold values from 1 to 512, 4096 in all
Outputs:
- query_grad: bfloat16 [8192, 4096], P(('parts', 'seq')), parts along dimension 0
- key_grad: bfloat16 [8192, 256], P(('parts', 'seq')), parts along dimension 0
- value_grad: bfloat16 [8192, 256], P(('parts', 'seq')), parts along dimension 0
There are 2 independent parts, one for each index of `parts`. A program takes and returns all parts, laid end to end along the dimension named above; each array names one. Nothing has to cross between parts.
Inputs may be any that keep to these rules, and one draw needn't show every extreme that they name: `doc_lengths`: lengths of whole documents that fill the pack: they sum to 4096, and the longest has exactly 512 tokens.
All inputs are finite; a program needn't handle non-finite values.
Results may differ from a plain program's by a relative error of at most 0.0057.
Values may be sent and summed in bfloat16 or wider, within the bound.
No kernel may reach another device: no remote copies, remote signals or barrier semaphores. Data moves between devices by JAX's collectives and lax.ppermute only.
A program may use at most 64 MiB of HBM per device.

v0:
```python
import math

import jax
import jax.numpy as jnp
from jax import lax
from jax.experimental import pallas as pl
from jax.experimental.pallas import tpu as pltpu
from jax.sharding import PartitionSpec as P

HD = 128
MOST = 512
KEY_TILE = 256
HEADS_PER_STEP = 8
NT_DIMS = (((1,), (1,)), ((), ()))


def shifted(block, axis, distance):
    devices = range(lax.axis_size(axis))
    route = [(i - distance, i) for i in devices if i - distance in devices]
    return lax.ppermute(block, axis, route)


def make_kernel(tok, reach, remote, dq_in, dq_final, n_alias):
    hb = HEADS_PER_STEP
    pieces = list(range(reach)) if remote else [reach]
    tiles_per_piece = tok // KEY_TILE
    n_rows = len(pieces) * tok
    scale = 1.0 / math.sqrt(HD)

    def kernel(flags_ref, q_ref, do_ref, o_ref, lse_ref, bias_ref, *rest):
        rest = list(rest)
        kv_refs = [rest.pop(0) for _ in pieces]
        dqp_ref = rest.pop(0) if dq_in else None
        rest = rest[n_alias:]
        dq_ref = rest.pop(0)
        dkv_refs = [rest.pop(0) for _ in pieces]
        qs_scr, dos_scr, dqt_scr, kt_scr, acc_scr = rest[-5:]
        b = pl.program_id(0)
        nb = pl.num_programs(0)

        @pl.when(b == 0)
        def _():
            acc_scr[...] = jnp.zeros_like(acc_scr)
            for n, kv in enumerate(kv_refs):
                kt_scr[:, n * tok:(n + 1) * tok] = (
                    kv[:, :HD].astype(jnp.float32).T.astype(jnp.bfloat16))

        delta_rows = []
        for i in range(hb):
            cols = slice(i * HD, (i + 1) * HD)
            qs_scr[i * tok:(i + 1) * tok, :] = q_ref[:, cols]
            dos_scr[i * tok:(i + 1) * tok, :] = do_ref[:, cols]
            prod = do_ref[:, cols].astype(jnp.float32) * o_ref[:, cols].astype(jnp.float32)
            delta_rows.append(jnp.sum(prod.T, axis=0, keepdims=True))
        dl_row = jnp.concatenate(delta_rows, axis=1)
        lse_row = jnp.concatenate([lse_ref[i:i + 1, :] for i in range(hb)], axis=1)
        dqt_scr[...] = jnp.zeros_like(dqt_scr)

        for n, piece in enumerate(pieces):
            kv = kv_refs[n]
            for t in range(tiles_per_piece):
                j = piece * tiles_per_piece + t
                rows = slice(t * KEY_TILE, (t + 1) * KEY_TILE)
                loc_rows = slice(n * tok + t * KEY_TILE, n * tok + (t + 1) * KEY_TILE)

                def tile(kv=kv, rows=rows, loc_rows=loc_rows, n=n):
                    k = kv[rows, :HD]
                    v = kv[rows, HD:]
                    qs = qs_scr[...]
                    dos = dos_scr[...]
                    st = lax.dot_general(k, qs, NT_DIMS, preferred_element_type=jnp.float32)
                    bias = bias_ref[loc_rows, :]
                    p = jnp.exp(st * scale - lse_row + jnp.concatenate([bias] * hb, axis=1))
                    dv = jnp.dot(p.astype(jnp.bfloat16), dos, preferred_element_type=jnp.float32)
                    dpt = lax.dot_general(v, dos, NT_DIMS, preferred_element_type=jnp.float32)
                    ds = (p * (dpt - dl_row)).astype(jnp.bfloat16)
                    dk = jnp.dot(ds, qs, preferred_element_type=jnp.float32)
                    acc_scr[n, rows, :HD] += dk
                    acc_scr[n, rows, HD:] += dv
                    dqt_scr[...] += jnp.dot(
                        kt_scr[:, loc_rows], ds, preferred_element_type=jnp.float32)

                if remote:
                    pl.when(flags_ref[j] != 0)(tile)
                else:
                    tile()

        for i in range(hb):
            cols = slice(i * HD, (i + 1) * HD)
            part = dqt_scr[:, i * tok:(i + 1) * tok].T
            if dq_in:
                part = part + dqp_ref[:, cols]
            if dq_final:
                dq_ref[:, cols] = (part * scale).astype(dq_ref.dtype)
            else:
                dq_ref[:, cols] = part

        @pl.when(b == nb - 1)
        def _():
            for n, dkv_ref in enumerate(dkv_refs):
                dkv_ref[...] = acc_scr[n].astype(dkv_ref.dtype)

    return kernel


def grads_call(group, remote, flags, queries, out_grad, outputs, lse, bias, kv_pieces,
               reach, dq_part=None, dq_alias=None, dkv_alias=None):
    tok, width = queries.shape
    n_heads = width // HD
    kvh = kv_pieces[0].shape[1] // (2 * HD)
    heads_per_group = n_heads // kvh
    hb = HEADS_PER_STEP
    nb = heads_per_group // hb
    dq_final = dq_part is not None
    pieces = list(range(reach)) if remote else [reach]
    n_pieces = len(pieces)

    def head_block(b, *f):
        return (0, group * nb + b)

    def lse_block(b, *f):
        return (group * nb + b, 0)

    def local_block(b, *f):
        return (0, b)

    def bias_block(b, *f):
        return (0, 0)

    def kv_block(b, *f):
        return (0, group)

    in_specs = [
        pl.BlockSpec((tok, hb * HD), head_block),
        pl.BlockSpec((tok, hb * HD), head_block),
        pl.BlockSpec((tok, hb * HD), head_block),
        pl.BlockSpec((hb, tok), lse_block),
        pl.BlockSpec((n_pieces * tok, tok), bias_block),
    ] + [pl.BlockSpec((tok, 2 * HD), kv_block) for _ in pieces]
    args = [queries, out_grad, outputs, lse, bias] + [kv_pieces[reach - p] for p in pieces]
    if dq_part is not None:
        in_specs.append(pl.BlockSpec((tok, hb * HD), local_block))
        args.append(dq_part)
    aliases = {}
    if dq_alias is not None:
        aliases[len(args) + int(remote)] = 0
        in_specs.append(pl.BlockSpec(memory_space=pl.ANY))
        args.append(dq_alias)
    if dkv_alias is not None:
        for n, piece_arr in enumerate(dkv_alias):
            aliases[len(args) + int(remote)] = 1 + n
            in_specs.append(pl.BlockSpec(memory_space=pl.ANY))
            args.append(piece_arr)

    kernel = make_kernel(tok, reach, remote, dq_part is not None, dq_final, len(aliases))
    if dq_final:
        dq_shape = jax.ShapeDtypeStruct((tok, width), jnp.bfloat16)
        dq_spec = pl.BlockSpec((tok, hb * HD), head_block)
    else:
        dq_shape = jax.ShapeDtypeStruct((tok, heads_per_group * HD), jnp.float32)
        dq_spec = pl.BlockSpec((tok, hb * HD), local_block)
    if remote:
        dkv_shape = jax.ShapeDtypeStruct((tok, kvh * 2 * HD), jnp.bfloat16)
        dkv_spec = pl.BlockSpec((tok, 2 * HD), lambda b, *f: (0, group))
    else:
        dkv_shape = jax.ShapeDtypeStruct((tok, kvh * 2 * HD), jnp.float32)
        dkv_spec = pl.BlockSpec((tok, 2 * HD), lambda b, *f: (0, group))

    if not remote:
        body = kernel

        def kernel(*refs):
            body(None, *refs)

    grid_spec = pltpu.PrefetchScalarGridSpec(
        num_scalar_prefetch=1 if remote else 0,
        grid=(nb,),
        in_specs=in_specs,
        out_specs=[dq_spec] + [dkv_spec] * n_pieces,
        scratch_shapes=[
            pltpu.VMEM((hb * tok, HD), jnp.bfloat16),
            pltpu.VMEM((hb * tok, HD), jnp.bfloat16),
            pltpu.VMEM((HD, hb * tok), jnp.float32),
            pltpu.VMEM((HD, n_pieces * tok), jnp.bfloat16),
            pltpu.VMEM((n_pieces, tok, 2 * HD), jnp.float32),
        ],
    )
    outs = pl.pallas_call(
        kernel,
        grid_spec=grid_spec,
        out_shape=[dq_shape] + [dkv_shape] * n_pieces,
        input_output_aliases=aliases,
        compiler_params=pltpu.CompilerParams(dimension_semantics=("arbitrary",)),
    )(*([flags] if remote else []), *args)
    return outs[0], outs[1:]


def per_device(queries, keys, values, outputs, out_grad, logsumexp, doc_lengths):
    tok, width = queries.shape
    kvh = keys.shape[1] // HD
    reach = -(-(MOST - 1) // tok)
    win = (reach + 1) * tok
    scale = 1.0 / math.sqrt(HD)
    position = lax.axis_index("seq")
    doc_ends = jnp.cumsum(doc_lengths)

    def doc_of(places):
        return jnp.sum((doc_ends[None, :] <= places[:, None]).astype(jnp.int32), axis=1)

    key_places = (position - reach) * tok + jnp.arange(win, dtype=jnp.int32)
    key_ids = jnp.where(key_places >= 0, doc_of(key_places), -1)
    query_ids = key_ids[reach * tok:]
    query_index = jnp.arange(tok, dtype=jnp.int32)
    own_visible = (query_ids[:, None] == query_ids[None, :]) & (
        query_index[:, None] <= query_index[None, :])
    bias_own = jnp.where(own_visible, 0.0, -jnp.inf).astype(jnp.float32)
    remote_ids = key_ids[:reach * tok]
    bias_rem = jnp.where(remote_ids[:, None] == query_ids[None, :], 0.0, -jnp.inf
                         ).astype(jnp.float32)
    n_tiles = win // KEY_TILE
    flags = (key_ids[KEY_TILE - 1::KEY_TILE] == query_ids[0]).astype(jnp.int32)

    kv = jnp.concatenate(
        [part for g in range(kvh)
         for part in (keys[:, g * HD:(g + 1) * HD], values[:, g * HD:(g + 1) * HD])], axis=1)
    kv_pieces = [kv] + [shifted(kv, "seq", hop) for hop in range(1, reach + 1)]
    own = (None, queries, out_grad, outputs, logsumexp, bias_own, kv_pieces, reach)
    rem = (flags, queries, out_grad, outputs, logsumexp, bias_rem, kv_pieces, reach)

    dq_part0, (dkv_own0,) = grads_call(0, False, *own)
    dq, dkv_rem = grads_call(0, True, *rem, dq_part=dq_part0)
    dq_part1, dkv_rem = grads_call(1, True, *rem, dkv_alias=dkv_rem)
    returned = [shifted(dkv_rem[reach - hop], "seq", -hop) for hop in range(1, reach + 1)]
    dq, (total,) = grads_call(1, False, *own, dq_part=dq_part1, dq_alias=dq,
                              dkv_alias=[dkv_own0])

    for r in returned:
        total = total + r.astype(jnp.float32)
    key_total = jnp.concatenate(
        [total[:, (2 * g) * HD:(2 * g + 1) * HD] for g in range(kvh)], axis=1)
    value_total = jnp.concatenate(
        [total[:, (2 * g + 1) * HD:(2 * g + 2) * HD] for g in range(kvh)], axis=1)
    return (
        dq,
        (key_total * scale).astype(jnp.bfloat16),
        value_total.astype(jnp.bfloat16),
    )


def solution(mesh):
    in_specs = (
        P(("parts", "seq"), None),
        P(("parts", "seq"), None),
        P(("parts", "seq"), None),
        P(("parts", "seq"), None),
        P(("parts", "seq"), None),
        P(None, ("parts", "seq")),
        P("parts"),
    )
    out_specs = (P(("parts", "seq"), None), P(("parts", "seq"), None), P(("parts", "seq"), None))
    return jax.shard_map(
        per_device, mesh=mesh, in_specs=in_specs, out_specs=out_specs, check_vma=False
    )
```

profile of v0, /device:TPU:14, one launch (start us, length us, event | category | flops | bytes accessed | tf_op | source)
XLA Modules:
  0.0 60.9 jit_solution(11559839003961212082)
XLA Ops:
  0.6 1.0 %fusion.6 = (bf16[256,128]{1,0:T(8,128)(2,1)S(1)}, bf16[256,128]{1,0:T(8,128)(2,1)S(1)}, bf16[256,128]{1,0:T(8,128)(2,1)S(1)}, bf16[256,128]{1,0:T(8,128)(2,1)S(1)}) fusion(bf16[256,256]{1,0:T(8,128)(2,1)} %param.8, bf16[256,256]{1,0:T(8,128)(2,1)} %param.9), kind=kLoop, calls=%fused_computation.16 | loop fusion | bytes 524288 | tf_op jit(solution)/shard_map/slice | solution.py:225
  1.6 0.0 copy-start
  1.6 1.9 %collective-permute-start.1 = (bf16[256,512]{1,0:T(8,128)(2,1)S(1)}, bf16[256,512]{1,0:T(8,128)(2,1)S(1)}, u32[]{:S(2)}, u32[]{:S(2)}) collective-permute-start(bf16[256,512]{1,0:T(8,128)(2,1)S(1)} %pad_maximum_fusion.refs_5_), channel_id=1, source_target_pairs={{0,1},{1,2},{2,3},{3,4},{4,5},{5,6},{6,7},{7,8},{8,9},{9,10},{10,1... | collective-permute-start | bytes 786440 | tf_op jit(solution)/shard_map/ppermute | solution.py:20
  3.6 3.4 %collective-permute-start = (bf16[256,512]{1,0:T(8,128)(2,1)S(1)}, bf16[256,512]{1,0:T(8,128)(2,1)S(1)}, u32[]{:S(2)}, u32[]{:S(2)}) collective-permute-start(bf16[256,512]{1,0:T(8,128)(2,1)S(1)} %pad_maximum_fusion.refs_5_), channel_id=1, source_target_pairs={{0,2},{1,3},{2,4},{3,5},{4,6},{5,7},{6,8},{7,9},{8,10},{9,11},{10,... | collective-permute-start | bytes 786440 | tf_op jit(solution)/shard_map/ppermute | solution.py:20
  7.0 0.7 %copy.16 = s32[16,1]{1,0:T(8,128)S(1)} copy(s32[16,1]{0,1:T(1,128)} %bitcast.2) | data formatting | bytes 128 | tf_op jit(solution)/shard_map/reshape.26
  7.8 0.1 reduce
  7.9 0.1 convert_reduce_fusion
  8.0 0.5 slice.45
  8.5 0.1 slice.44
  8.6 0.8 %fusion.2.refs_4_ = f32[256,256]{1,0:T(8,128)} fusion(s32[256]{0:T(256)S(1)} %slice.39), kind=kLoop, calls=%fused_computation.7 | loop fusion | flops 262144 | bytes 263168 | tf_op jit(solution)/shard_map/jit(_where)/select_n | solution.py:216
  9.4 1.2 %compare_convert_fusion.flags_ref = s32[3]{0:T(128)} fusion(s32[3]{0:T(128)S(1)} %slice.44, s32[]{:T(128)} %bitcast.1), kind=kLoop, calls=%fused_computation.12 | loop fusion | flops 6 | bytes 28 | tf_op jit(solution)/shard_map/convert_element_type | solution.py:221
  10.6 0.0 copy-done
  10.6 6.8 %shard_map.94 = (f32[256,2048]{1,0:T(8,128)}, f32[256,512]{1,0:T(8,128)}) custom-call(bf16[256,4096]{1,0:T(8,128)(2,1)} %refs_0_.3, bf16[256,4096]{1,0:T(8,128)(2,1)} %refs_1_.3, bf16[256,4096]{1,0:T(8,128)(2,1)} %refs_2_.3, f32[32,256]{1,0:T(8,128)} %refs_3_.3, f32[256,256]{1,0:T(8,128)} %fusion.2.refs_4_, bf16[256,512]{1,0:T(8,128)(2,1)} %copy-done), custom_call_target="tpu_custom_call" | custom-call | tf_op jit(solution)/shard_map/pallas_call | solution.py:188
  17.4 0.9 %compare_select_fusion.bias_ref = f32[512,256]{1,0:T(8,128)} fusion(s32[256]{0:T(256)S(1)} %slice.39, s32[512]{0:T(512)S(1)} %slice.46), kind=kLoop, calls=%fused_computation.1 | loop fusion | flops 262144 | bytes 527360 | tf_op jit(solution)/shard_map/jit(_where)/select_n | solution.py:218
  18.3 0.0 collective-permute-done.1.rest_1_
  18.3 0.0 copy-start.1
  18.3 0.0 collective-permute-done.rest_0_
  18.4 0.0 copy-start.2
  18.4 0.7 %copy-done.1 = bf16[256,512]{1,0:T(8,128)(2,1)} copy-done((bf16[256,512]{1,0:T(8,128)(2,1)}, bf16[256,512]{1,0:T(8,128)(2,1)S(1)}, u32[]{:S(2)}) %copy-start.1) | copy-done | bytes 262168
  19.0 0.1 copy-done.2
  19.1 8.6 %shard_map.95 = (bf16[256,4096]{1,0:T(8,128)(2,1)}, bf16[256,512]{1,0:T(8,128)(2,1)}, bf16[256,512]{1,0:T(8,128)(2,1)}) custom-call(s32[3]{0:T(128)} %compare_convert_fusion.flags_ref, bf16[256,4096]{1,0:T(8,128)(2,1)} %refs_0_.3, bf16[256,4096]{1,0:T(8,128)(2,1)} %refs_1_.3, bf16[256,4096]{1,0:T(8,128)(2,1)} %refs_2_.3, f32[32,256]{1,0:T(8,128)} %refs_3_.3, ...), custom_call_target="tpu_custom_call" | custom-call | tf_op jit(solution)/shard_map/pallas_call | solution.py:188
  27.8 8.5 %shard_map.96 = (f32[256,2048]{1,0:T(8,128)}, bf16[256,512]{1,0:T(8,128)(2,1)}, bf16[256,512]{1,0:T(8,128)(2,1)}) custom-call(s32[3]{0:T(128)} %compare_convert_fusion.flags_ref, bf16[256,4096]{1,0:T(8,128)(2,1)} %refs_0_.3, bf16[256,4096]{1,0:T(8,128)(2,1)} %refs_1_.3, bf16[256,4096]{1,0:T(8,128)(2,1)} %refs_2_.3, ...), custom_call_target="tpu_custom_call", output_to_operand_aliasing={{1}: (8, {}), {2}: (9, {})} | custom-call | tf_op jit(solution)/shard_map/pallas_call | solution.py:188
  36.3 3.4 %collective-permute-start.2 = (bf16[256,512]{1,0:T(8,128)(2,1)}, bf16[256,512]{1,0:T(8,128)(2,1)S(1)}, u32[]{:S(2)}, u32[]{:S(2)}) collective-permute-start(bf16[256,512]{1,0:T(8,128)(2,1)} %get-tuple-element.21), channel_id=1, source_target_pairs={{1,0},{2,1},{3,2},{4,3},{5,4},{6,5},{7,6},{8,7},{9,8},{10,9},{11,1... | collective-permute-start | bytes 786440 | tf_op jit(solution)/shard_map/ppermute | solution.py:20
  39.7 3.3 %collective-permute-start.3 = (bf16[256,512]{1,0:T(8,128)(2,1)}, bf16[256,512]{1,0:T(8,128)(2,1)S(1)}, u32[]{:S(2)}, u32[]{:S(2)}) collective-permute-start(bf16[256,512]{1,0:T(8,128)(2,1)} %get-tuple-element.22), channel_id=1, source_target_pairs={{2,0},{3,1},{4,2},{5,3},{6,4},{7,5},{8,6},{9,7},{10,8},{11,9},{12,... | collective-permute-start | bytes 786440 | tf_op jit(solution)/shard_map/ppermute | solution.py:20
  43.0 6.9 %shard_map.97 = (bf16[256,4096]{1,0:T(8,128)(2,1)}, f32[256,512]{1,0:T(8,128)}) custom-call(bf16[256,4096]{1,0:T(8,128)(2,1)} %refs_0_.3, bf16[256,4096]{1,0:T(8,128)(2,1)} %refs_1_.3, bf16[256,4096]{1,0:T(8,128)(2,1)} %refs_2_.3, f32[32,256]{1,0:T(8,128)} %refs_3_.3, f32[256,256]{1,0:T(8,128)} %fusion.2.refs_4_, ...), custom_call_target="tpu_custom_call", output_to_operand_aliasing={{0}: (7, {}), {1}: (8, {})} | custom-call | tf_op jit(solution)/shard_map/pallas_call | solution.py:188
  49.9 0.0 collective-permute-done.2
  49.9 8.4 %collective-permute-done.3 = bf16[256,512]{1,0:T(8,128)(2,1)S(1)} collective-permute-done((bf16[256,512]{1,0:T(8,128)(2,1)}, bf16[256,512]{1,0:T(8,128)(2,1)S(1)}, u32[]{:S(2)}, u32[]{:S(2)}) %collective-permute-start.3) | collective-permute-done | bytes 262176 | tf_op jit(solution)/shard_map/ppermute | solution.py:20
  58.3 1.1 %fusion.3 = (bf16[256,512]{1,0:T(8,128)(2,1)S(1)}, f32[256,512]{1,0:T(8,128)S(1)}) fusion(bf16[256,512]{1,0:T(8,128)(2,1)S(1)} %collective-permute-done.3, f32[256,512]{1,0:T(8,128)} %get-tuple-element.20, bf16[256,512]{1,0:T(8,128)(2,1)S(1)} %collective-permute-done.2), kind=kLoop, calls=%fused_computation.13 | loop fusion | flops 655360 | bytes 1835008 | tf_op jit(solution)/shard_map/convert.3
  59.5 0.7 %pad_maximum_fusion.1 = bf16[256,256]{1,0:T(8,128)(2,1)} fusion(bf16[256,128]{1,0:T(8,128)(2,1)S(1)} %get-tuple-element.28, bf16[256,128]{1,0:T(8,128)(2,1)S(1)} %get-tuple-element.27), kind=kLoop, calls=%fused_computation.8 | loop fusion | flops 262144 | bytes 262144 | tf_op jit(solution)/shard_map/concatenate | solution.py:241
  60.2 0.7 %fusion = bf16[256,256]{1,0:T(8,128)(2,1)} fusion(f32[256,128]{1,0:T(8,128)S(1)} %get-tuple-element.26, f32[256,128]{1,0:T(8,128)S(1)} %get-tuple-element.25), kind=kLoop, calls=%fused_computation.4 | loop fusion | flops 196608 | bytes 393216 | tf_op jit(solution)/shard_map/convert_element_type | solution.py:245
  (8 shorter events, 0.1 us)
Async XLA Ops:
  1.6 9.0 %copy-start = (bf16[256,512]{1,0:T(8,128)(2,1)}, bf16[256,512]{1,0:T(8,128)(2,1)S(1)}, u32[]{:S(2)}) copy-start(bf16[256,512]{1,0:T(8,128)(2,1)S(1)} %pad_maximum_fusion.refs_5_) | copy-start | bytes 786436
  1.6 16.7 %collective-permute-start.1 = (bf16[256,512]{1,0:T(8,128)(2,1)S(1)}, bf16[256,512]{1,0:T(8,128)(2,1)S(1)}, u32[]{:S(2)}, u32[]{:S(2)}) collective-permute-start(bf16[256,512]{1,0:T(8,128)(2,1)S(1)} %pad_maximum_fusion.refs_5_), channel_id=1, source_target_pairs={{0,1},{1,2},{2,3},{3,4},{4,5},{5,6},{6,7},{7,8},{8,9},{9,10},{10,1... | collective-permute-start | bytes 786440 | tf_op jit(solution)/shard_map/ppermute | solution.py:20
  3.6 14.8 %collective-permute-start = (bf16[256,512]{1,0:T(8,128)(2,1)S(1)}, bf16[256,512]{1,0:T(8,128)(2,1)S(1)}, u32[]{:S(2)}, u32[]{:S(2)}) collective-permute-start(bf16[256,512]{1,0:T(8,128)(2,1)S(1)} %pad_maximum_fusion.refs_5_), channel_id=1, source_target_pairs={{0,2},{1,3},{2,4},{3,5},{4,6},{5,7},{6,8},{7,9},{8,10},{9,11},{10,... | collective-permute-start | bytes 786440 | tf_op jit(solution)/shard_map/ppermute | solution.py:20
  18.3 0.7 %copy-start.1 = (bf16[256,512]{1,0:T(8,128)(2,1)}, bf16[256,512]{1,0:T(8,128)(2,1)S(1)}, u32[]{:S(2)}) copy-start(bf16[256,512]{1,0:T(8,128)(2,1)S(1)} %collective-permute-done.1.rest_1_) | copy-start | bytes 786436
  18.4 0.8 %copy-start.2 = (bf16[256,512]{1,0:T(8,128)(2,1)}, bf16[256,512]{1,0:T(8,128)(2,1)S(1)}, u32[]{:S(2)}) copy-start(bf16[256,512]{1,0:T(8,128)(2,1)S(1)} %collective-permute-done.rest_0_) | copy-start | bytes 786436
  36.3 13.6 %collective-permute-start.2 = (bf16[256,512]{1,0:T(8,128)(2,1)}, bf16[256,512]{1,0:T(8,128)(2,1)S(1)}, u32[]{:S(2)}, u32[]{:S(2)}) collective-permute-start(bf16[256,512]{1,0:T(8,128)(2,1)} %get-tuple-element.21), channel_id=1, source_target_pairs={{1,0},{2,1},{3,2},{4,3},{5,4},{6,5},{7,6},{8,7},{9,8},{10,9},{11,1... | collective-permute-start | bytes 786440 | tf_op jit(solution)/shard_map/ppermute | solution.py:20
  39.7 18.7 %collective-permute-start.3 = (bf16[256,512]{1,0:T(8,128)(2,1)}, bf16[256,512]{1,0:T(8,128)(2,1)S(1)}, u32[]{:S(2)}, u32[]{:S(2)}) collective-permute-start(bf16[256,512]{1,0:T(8,128)(2,1)} %get-tuple-element.22), channel_id=1, source_target_pairs={{2,0},{3,1},{4,2},{5,3},{6,4},{7,5},{8,6},{9,7},{10,8},{11,9},{12,... | collective-permute-start | bytes 786440 | tf_op jit(solution)/shard_map/ppermute | solution.py:20
where the time goes:
time: 61.2 us; the launch traced here: 60.9 us
  Pallas kernels  30.8 us (50%)
  starting transfers between devices  12 us (20%)
  waiting for transfers between devices  8.45 us (14%)
  other arithmetic  5.69 us (9%)
  local copies, waits for them, and re-layouts  3.12 us (5%)
  between operations  0.75 us (1%)
    pallas_call x4, Pallas kernels, grads_call(): pl.pallas_call(kernel, grid_spec=grid_spec, out_shape=[dq_shape] + [dkv_s...  30.8 us
    ppermute x4, starting transfers between devices, shifted(): return lax.ppermute(block, axis, route)  12 us
    ppermute x4, waiting for transfers between devices, shifted(): return lax.ppermute(block, axis, route)  8.45 us
    another operation x3, other arithmetic  1.3 us
  transfers between devices with their start and end apart: 4, of which 1 were waited for; matrix products, arithmetic and copies ran while one was open for 7% of the time, Pallas kernels for 22%

commit v1 on v0

--- a/solution.py
+++ b/solution.py
@@ -20,9 +20,8 @@
     return lax.ppermute(block, axis, route)
 
 
-def make_kernel(tok, reach, remote, dq_in, dq_final, n_alias):
+def make_kernel(tok, pieces, remote, dq_in, dq_final, n_alias):
     hb = HEADS_PER_STEP
-    pieces = list(range(reach)) if remote else [reach]
     tiles_per_piece = tok // KEY_TILE
     n_rows = len(pieces) * tok
     scale = 1.0 / math.sqrt(HD)
@@ -103,16 +102,15 @@
     return kernel
 
 
-def grads_call(group, remote, flags, queries, out_grad, outputs, lse, bias, kv_pieces,
-               reach, dq_part=None, dq_alias=None, dkv_alias=None):
+def grads_call(group, pieces, flags, queries, out_grad, outputs, lse, bias, kv_pieces,
+               reach, dq_part=None, dq_final=False, dq_alias=None, dkv_alias=None):
+    remote = pieces[0] < reach
     tok, width = queries.shape
     n_heads = width // HD
     kvh = kv_pieces[0].shape[1] // (2 * HD)
     heads_per_group = n_heads // kvh
     hb = HEADS_PER_STEP
     nb = heads_per_group // hb
-    dq_final = dq_part is not None
-    pieces = list(range(reach)) if remote else [reach]
     n_pieces = len(pieces)
 
     def head_block(b, *f):
@@ -125,7 +123,7 @@
         return (0, b)
 
     def bias_block(b, *f):
-        return (0, 0)
+        return (pieces[0], 0) if remote else (0, 0)
 
     def kv_block(b, *f):
         return (0, group)
@@ -152,7 +150,7 @@
             in_specs.append(pl.BlockSpec(memory_space=pl.ANY))
             args.append(piece_arr)
 
-    kernel = make_kernel(tok, reach, remote, dq_part is not None, dq_final, len(aliases))
+    kernel = make_kernel(tok, pieces, remote, dq_part is not None, dq_final, len(aliases))
     if dq_final:
         dq_shape = jax.ShapeDtypeStruct((tok, width), jnp.bfloat16)
         dq_spec = pl.BlockSpec((tok, hb * HD), head_block)
@@ -227,11 +225,22 @@
     own = (None, queries, out_grad, outputs, logsumexp, bias_own, kv_pieces, reach)
     rem = (flags, queries, out_grad, outputs, logsumexp, bias_rem, kv_pieces, reach)
 
-    dq_part0, (dkv_own0,) = grads_call(0, False, *own)
-    dq, dkv_rem = grads_call(0, True, *rem, dq_part=dq_part0)
-    dq_part1, dkv_rem = grads_call(1, True, *rem, dkv_alias=dkv_rem)
-    returned = [shifted(dkv_rem[reach - hop], "seq", -hop) for hop in range(1, reach + 1)]
-    dq, (total,) = grads_call(1, False, *own, dq_part=dq_part1, dq_alias=dq,
+    dq_part0, (dkv_own0,) = grads_call(0, [reach], *own)
+    dq_part1 = None
+    dq = None
+    returned = []
+    for piece in range(reach):
+        last = piece == reach - 1
+        dq0, piece0 = grads_call(0, [piece], *rem, dq_part=dq_part0, dq_final=last)
+        dq_part1, piece_all = grads_call(1, [piece], *rem, dq_part=dq_part1,
+                                         dkv_alias=piece0)
+        if last:
+            dq = dq0
+        else:
+            dq_part0 = dq0
+        returned.append(shifted(piece_all[0], "seq", piece - reach))
+    returned = returned[::-1]
+    dq, (total,) = grads_call(1, [reach], *own, dq_part=dq_part1, dq_final=True, dq_alias=dq,
                               dkv_alias=[dkv_own0])
 
     for r in returned:

time: 61.2 us -> 70.5 us (1.15)
  the two profiles are of different devices: /device:TPU:14 before, /device:TPU:18 now
where the time goes in v1:
time: 70.5 us; the launch traced here: 70 us
  Pallas kernels  41.6 us (59%)
  starting transfers between devices  18.3 us (26%)
  other arithmetic  5.7 us (8%)
  local copies, waits for them, and re-layouts  3.71 us (5%)
  between operations  0.77 us (1%)
    pallas_call x6, Pallas kernels, grads_call(): pl.pallas_call(kernel, grid_spec=grid_spec, out_shape=[dq_shape] + [dkv_s...  41.6 us
    ppermute x4, starting transfers between devices, shifted(): return lax.ppermute(block, axis, route)  18.3 us
  transfers between devices with their start and end apart: 4, of which 0 were waited for; matrix products, arithmetic and copies ran while one was open for 6% of the time, Pallas kernels for 59%

profile of v1, /device:TPU:18, one launch (start us, length us, event | category | flops | bytes accessed | tf_op | source)
XLA Modules:
  0.0 70.0 jit_solution(11761898487590554391)
XLA Ops:
  0.6 1.0 %fusion.6 = (bf16[256,128]{1,0:T(8,128)(2,1)S(1)}, bf16[256,128]{1,0:T(8,128)(2,1)S(1)}, bf16[256,128]{1,0:T(8,128)(2,1)S(1)}, bf16[256,128]{1,0:T(8,128)(2,1)S(1)}) fusion(bf16[256,256]{1,0:T(8,128)(2,1)} %param.8, bf16[256,256]{1,0:T(8,128)(2,1)} %param.9), kind=kLoop, calls=%fused_computation.16 | loop fusion | bytes 524288 | tf_op jit(solution)/shard_map/slice | solution.py:223
  1.6 0.0 copy-start
  1.6 3.4 %collective-permute-start.1 = (bf16[256,512]{1,0:T(8,128)(2,1)S(1)}, bf16[256,512]{1,0:T(8,128)(2,1)S(1)}, u32[]{:S(2)}, u32[]{:S(2)}) collective-permute-start(bf16[256,512]{1,0:T(8,128)(2,1)S(1)} %pad_maximum_fusion.refs_5_), channel_id=1, source_target_pairs={{0,2},{1,3},{2,4},{3,5},{4,6},{5,7},{6,8},{7,9},{8,10},{9,11},{10,... | collective-permute-start | bytes 786440 | tf_op jit(solution)/shard_map/ppermute | solution.py:20
  5.1 1.9 %collective-permute-start = (bf16[256,512]{1,0:T(8,128)(2,1)S(1)}, bf16[256,512]{1,0:T(8,128)(2,1)S(1)}, u32[]{:S(2)}, u32[]{:S(2)}) collective-permute-start(bf16[256,512]{1,0:T(8,128)(2,1)S(1)} %pad_maximum_fusion.refs_5_), channel_id=1, source_target_pairs={{0,1},{1,2},{2,3},{3,4},{4,5},{5,6},{6,7},{7,8},{8,9},{9,10},{10,1... | collective-permute-start | bytes 786440 | tf_op jit(solution)/shard_map/ppermute | solution.py:20
  7.0 0.7 %copy.16 = s32[16,1]{1,0:T(8,128)S(1)} copy(s32[16,1]{0,1:T(1,128)} %bitcast.2) | data formatting | bytes 128 | tf_op jit(solution)/shard_map/reshape.26
  7.8 0.1 reduce
  7.9 0.1 convert_reduce_fusion
  8.0 0.5 slice.45
  8.5 0.1 slice.44
  8.6 0.8 %fusion.2.refs_4_ = f32[256,256]{1,0:T(8,128)} fusion(s32[256]{0:T(256)S(1)} %slice.39), kind=kLoop, calls=%fused_computation.7 | loop fusion | flops 262144 | bytes 263168 | tf_op jit(solution)/shard_map/jit(_where)/select_n | solution.py:214
  9.5 1.2 %compare_convert_fusion.flags_ref = s32[3]{0:T(128)} fusion(s32[3]{0:T(128)S(1)} %slice.44, s32[]{:T(128)} %bitcast.1), kind=kLoop, calls=%fused_computation.12 | loop fusion | flops 6 | bytes 28 | tf_op jit(solution)/shard_map/convert_element_type | solution.py:219
  10.6 0.0 copy-done
  10.6 6.7 %shard_map.94 = (f32[256,2048]{1,0:T(8,128)}, f32[256,512]{1,0:T(8,128)}) custom-call(bf16[256,4096]{1,0:T(8,128)(2,1)} %refs_0_.3, bf16[256,4096]{1,0:T(8,128)(2,1)} %refs_1_.3, bf16[256,4096]{1,0:T(8,128)(2,1)} %refs_2_.3, f32[32,256]{1,0:T(8,128)} %refs_3_.3, f32[256,256]{1,0:T(8,128)} %fusion.2.refs_4_, bf16[256,512]{1,0:T(8,128)(2,1)} %copy-done), custom_call_target="tpu_custom_call" | custom-call | tf_op jit(solution)/shard_map/pallas_call | solution.py:186
  17.3 0.9 %compare_select_fusion.bias_ref = f32[512,256]{1,0:T(8,128)} fusion(s32[256]{0:T(256)S(1)} %slice.39, s32[512]{0:T(512)S(1)} %slice.46), kind=kLoop, calls=%fused_computation.1 | loop fusion | flops 262144 | bytes 527360 | tf_op jit(solution)/shard_map/jit(_where)/select_n | solution.py:216
  18.2 0.0 collective-permute-done.1.rest_0_
  18.2 0.0 copy-start.2
  18.2 0.7 copy-done.2
  18.9 5.6 %shard_map.95 = (f32[256,2048]{1,0:T(8,128)}, bf16[256,512]{1,0:T(8,128)(2,1)}) custom-call(s32[3]{0:T(128)} %compare_convert_fusion.flags_ref, bf16[256,4096]{1,0:T(8,128)(2,1)} %refs_0_.3, bf16[256,4096]{1,0:T(8,128)(2,1)} %refs_1_.3, bf16[256,4096]{1,0:T(8,128)(2,1)} %refs_2_.3, f32[32,256]{1,0:T(8,128)} %refs_3_.3, ...), custom_call_target="tpu_custom_call" | custom-call | tf_op jit(solution)/shard_map/pallas_call | solution.py:186
  24.5 5.3 %shard_map.96 = (f32[256,2048]{1,0:T(8,128)}, bf16[256,512]{1,0:T(8,128)(2,1)}) custom-call(s32[3]{0:T(128)} %compare_convert_fusion.flags_ref, bf16[256,4096]{1,0:T(8,128)(2,1)} %refs_0_.3, bf16[256,4096]{1,0:T(8,128)(2,1)} %refs_1_.3, bf16[256,4096]{1,0:T(8,128)(2,1)} %refs_2_.3, f32[32,256]{1,0:T(8,128)} %refs_3_.3, ...), custom_call_target="tpu_custom_call", output_to_operand_aliasing={{1}: (7, {})} | custom-call | tf_op jit(solution)/shard_map/pallas_call | solution.py:186
  29.8 3.5 %collective-permute-start.3 = (bf16[256,512]{1,0:T(8,128)(2,1)}, bf16[256,512]{1,0:T(8,128)(2,1)S(1)}, u32[]{:S(2)}, u32[]{:S(2)}) collective-permute-start(bf16[256,512]{1,0:T(8,128)(2,1)} %get-tuple-element.26), channel_id=1, source_target_pairs={{2,0},{3,1},{4,2},{5,3},{6,4},{7,5},{8,6},{9,7},{10,8},{11,9},{12,... | collective-permute-start | bytes 786440 | tf_op jit(solution)/shard_map/ppermute | solution.py:20
  33.3 0.0 collective-permute-done.rest_0_
  33.3 0.0 copy-start.1
  33.3 0.7 copy-done.1
  34.0 8.4 %shard_map.97 = (bf16[256,4096]{1,0:T(8,128)(2,1)}, bf16[256,512]{1,0:T(8,128)(2,1)}) custom-call(s32[3]{0:T(128)} %compare_convert_fusion.flags_ref, bf16[256,4096]{1,0:T(8,128)(2,1)} %refs_0_.3, bf16[256,4096]{1,0:T(8,128)(2,1)} %refs_1_.3, bf16[256,4096]{1,0:T(8,128)(2,1)} %refs_2_.3, f32[32,256]{1,0:T(8,128)} %refs_3_.3, ...), custom_call_target="tpu_custom_call" | custom-call | tf_op jit(solution)/shard_map/pallas_call | solution.py:186
  42.4 8.7 %shard_map.98 = (f32[256,2048]{1,0:T(8,128)}, bf16[256,512]{1,0:T(8,128)(2,1)}) custom-call(s32[3]{0:T(128)} %compare_convert_fusion.flags_ref, bf16[256,4096]{1,0:T(8,128)(2,1)} %refs_0_.3, bf16[256,4096]{1,0:T(8,128)(2,1)} %refs_1_.3, bf16[256,4096]{1,0:T(8,128)(2,1)} %refs_2_.3, f32[32,256]{1,0:T(8,128)} %refs_3_.3, ...), custom_call_target="tpu_custom_call", output_to_operand_aliasing={{1}: (8, {})} | custom-call | tf_op jit(solution)/shard_map/pallas_call | solution.py:186
  51.1 9.4 %collective-permute-start.2 = (bf16[256,512]{1,0:T(8,128)(2,1)}, bf16[256,512]{1,0:T(8,128)(2,1)S(1)}, u32[]{:S(2)}, u32[]{:S(2)}) collective-permute-start(bf16[256,512]{1,0:T(8,128)(2,1)} %get-tuple-element.25), channel_id=1, source_target_pairs={{1,0},{2,1},{3,2},{4,3},{5,4},{6,5},{7,6},{8,7},{9,8},{10,9},{11,1... | collective-permute-start | bytes 786440 | tf_op jit(solution)/shard_map/ppermute | solution.py:20
  60.5 6.9 %shard_map.99 = (bf16[256,4096]{1,0:T(8,128)(2,1)}, f32[256,512]{1,0:T(8,128)}) custom-call(bf16[256,4096]{1,0:T(8,128)(2,1)} %refs_0_.3, bf16[256,4096]{1,0:T(8,128)(2,1)} %refs_1_.3, bf16[256,4096]{1,0:T(8,128)(2,1)} %refs_2_.3, f32[32,256]{1,0:T(8,128)} %refs_3_.3, f32[256,256]{1,0:T(8,128)} %fusion.2.refs_4_, ...), custom_call_target="tpu_custom_call", output_to_operand_aliasing={{0}: (7, {}), {1}: (8, {})} | custom-call | tf_op jit(solution)/shard_map/pallas_call | solution.py:186
  67.5 0.0 collective-permute-done.3
  67.5 0.0 collective-permute-done.2
  67.5 1.1 %fusion.3 = (bf16[256,512]{1,0:T(8,128)(2,1)S(1)}, f32[256,512]{1,0:T(8,128)S(1)}) fusion(bf16[256,512]{1,0:T(8,128)(2,1)S(1)} %collective-permute-done.3, f32[256,512]{1,0:T(8,128)} %get-tuple-element.24, bf16[256,512]{1,0:T(8,128)(2,1)S(1)} %collective-permute-done.2), kind=kLoop, calls=%fused_computation.13 | loop fusion | flops 655360 | bytes 1835008 | tf_op jit(solution)/shard_map/convert.3
  68.7 0.7 pad_maximum_fusion.1
  69.3 0.7 fusion
  (8 shorter events, 0.1 us)
Async XLA Ops:
  1.6 9.0 %copy-start = (bf16[256,512]{1,0:T(8,128)(2,1)}, bf16[256,512]{1,0:T(8,128)(2,1)S(1)}, u32[]{:S(2)}) copy-start(bf16[256,512]{1,0:T(8,128)(2,1)S(1)} %pad_maximum_fusion.refs_5_) | copy-start | bytes 786436
  1.6 16.6 %collective-permute-start.1 = (bf16[256,512]{1,0:T(8,128)(2,1)S(1)}, bf16[256,512]{1,0:T(8,128)(2,1)S(1)}, u32[]{:S(2)}, u32[]{:S(2)}) collective-permute-start(bf16[256,512]{1,0:T(8,128)(2,1)S(1)} %pad_maximum_fusion.refs_5_), channel_id=1, source_target_pairs={{0,2},{1,3},{2,4},{3,5},{4,6},{5,7},{6,8},{7,9},{8,10},{9,11},{10,... | collective-permute-start | bytes 786440 | tf_op jit(solution)/shard_map/ppermute | solution.py:20
  5.1 28.2 %collective-permute-start = (bf16[256,512]{1,0:T(8,128)(2,1)S(1)}, bf16[256,512]{1,0:T(8,128)(2,1)S(1)}, u32[]{:S(2)}, u32[]{:S(2)}) collective-permute-start(bf16[256,512]{1,0:T(8,128)(2,1)S(1)} %pad_maximum_fusion.refs_5_), channel_id=1, source_target_pairs={{0,1},{1,2},{2,3},{3,4},{4,5},{5,6},{6,7},{7,8},{8,9},{9,10},{10,1... | collective-permute-start | bytes 786440 | tf_op jit(solution)/shard_map/ppermute | solution.py:20
  18.2 0.7 copy-start.2
  29.8 37.7 %collective-permute-start.3 = (bf16[256,512]{1,0:T(8,128)(2,1)}, bf16[256,512]{1,0:T(8,128)(2,1)S(1)}, u32[]{:S(2)}, u32[]{:S(2)}) collective-permute-start(bf16[256,512]{1,0:T(8,128)(2,1)} %get-tuple-element.26), channel_id=1, source_target_pairs={{2,0},{3,1},{4,2},{5,3},{6,4},{7,5},{8,6},{9,7},{10,8},{11,9},{12,... | collective-permute-start | bytes 786440 | tf_op jit(solution)/shard_map/ppermute | solution.py:20
  33.3 0.7 copy-start.1
  51.1 16.4 %collective-permute-start.2 = (bf16[256,512]{1,0:T(8,128)(2,1)}, bf16[256,512]{1,0:T(8,128)(2,1)S(1)}, u32[]{:S(2)}, u32[]{:S(2)}) collective-permute-start(bf16[256,512]{1,0:T(8,128)(2,1)} %get-tuple-element.25), channel_id=1, source_target_pairs={{1,0},{2,1},{3,2},{4,3},{5,4},{6,5},{7,6},{8,7},{9,8},{10,9},{11,1... | collective-permute-start | bytes 786440 | tf_op jit(solution)/shard_map/ppermute | solution.py:20

commit v2 on v0

--- a/solution.py
+++ b/solution.py
@@ -80,10 +80,7 @@
                     dqt_scr[...] += jnp.dot(
                         kt_scr[:, loc_rows], ds, preferred_element_type=jnp.float32)
 
-                if remote:
-                    pl.when(flags_ref[j] != 0)(tile)
-                else:
-                    tile()
+                tile()
 
         for i in range(hb):
             cols = slice(i * HD, (i + 1) * HD)
@@ -143,12 +140,12 @@
         args.append(dq_part)
     aliases = {}
     if dq_alias is not None:
-        aliases[len(args) + int(remote)] = 0
+        aliases[len(args)] = 0
         in_specs.append(pl.BlockSpec(memory_space=pl.ANY))
         args.append(dq_alias)
     if dkv_alias is not None:
         for n, piece_arr in enumerate(dkv_alias):
-            aliases[len(args) + int(remote)] = 1 + n
+            aliases[len(args)] = 1 + n
             in_specs.append(pl.BlockSpec(memory_space=pl.ANY))
             args.append(piece_arr)
 
@@ -166,14 +163,13 @@
         dkv_shape = jax.ShapeDtypeStruct((tok, kvh * 2 * HD), jnp.float32)
         dkv_spec = pl.BlockSpec((tok, 2 * HD), lambda b, *f: (0, group))
 
-    if not remote:
-        body = kernel
-
-        def kernel(*refs):
-            body(None, *refs)
+    body = kernel
+
+    def kernel(*refs):
+        body(None, *refs)
 
     grid_spec = pltpu.PrefetchScalarGridSpec(
-        num_scalar_prefetch=1 if remote else 0,
+        num_scalar_prefetch=0,
         grid=(nb,),
         in_specs=in_specs,
         out_specs=[dq_spec] + [dkv_spec] * n_pieces,
@@ -191,7 +187,7 @@
         out_shape=[dq_shape] + [dkv_shape] * n_pieces,
         input_output_aliases=aliases,
         compiler_params=pltpu.CompilerParams(dimension_semantics=("arbitrary",)),
-    )(*([flags] if remote else []), *args)
+    )(*args)
     return outs[0], outs[1:]
 
 
@@ -217,15 +213,13 @@
     remote_ids = key_ids[:reach * tok]
     bias_rem = jnp.where(remote_ids[:, None] == query_ids[None, :], 0.0, -jnp.inf
                          ).astype(jnp.float32)
-    n_tiles = win // KEY_TILE
-    flags = (key_ids[KEY_TILE - 1::KEY_TILE] == query_ids[0]).astype(jnp.int32)
 
     kv = jnp.concatenate(
         [part for g in range(kvh)
          for part in (keys[:, g * HD:(g + 1) * HD], values[:, g * HD:(g + 1) * HD])], axis=1)
     kv_pieces = [kv] + [shifted(kv, "seq", hop) for hop in range(1, reach + 1)]
     own = (None, queries, out_grad, outputs, logsumexp, bias_own, kv_pieces, reach)
-    rem = (flags, queries, out_grad, outputs, logsumexp, bias_rem, kv_pieces, reach)
+    rem = (None, queries, out_grad, outputs, logsumexp, bias_rem, kv_pieces, reach)
 
     dq_part0, (dkv_own0,) = grads_call(0, False, *own)
     dq, dkv_rem = grads_call(0, True, *rem, dq_part=dq_part0)

time: 61.2 us -> 56.3 us (0.920)
  the two profiles are of different devices: /device:TPU:14 before, /device:TPU:12 now
where the time goes in v2:
time: 56.3 us; the launch traced here: 55.4 us
  Pallas kernels  33.2 us (59%)
  starting transfers between devices  12 us (21%)
  other arithmetic  4.53 us (8%)
  local copies, waits for them, and re-layouts  2.52 us (4%)
  waiting for transfers between devices  2.36 us (4%)
  between operations  0.76 us (1%)
    pallas_call x4, Pallas kernels, grads_call(): pl.pallas_call(kernel, grid_spec=grid_spec, out_shape=[dq_shape] + [dkv_s...  33.2 us
    ppermute x4, starting transfers between devices, shifted(): return lax.ppermute(block, axis, route)  12 us
    ppermute x4, waiting for transfers between devices, shifted(): return lax.ppermute(block, axis, route)  2.36 us
    another operation x3, other arithmetic  1.3 us
  transfers between devices with their start and end apart: 4, of which 1 were waited for; matrix products, arithmetic and copies ran while one was open for 5% of the time, Pallas kernels for 25%

profile of v2, /device:TPU:12, one launch (start us, length us, event | category | flops | bytes accessed | tf_op | source)
XLA Modules:
  0.0 55.4 jit_solution(661786292097455059)
XLA Ops:
  0.6 1.0 %fusion.6 = (bf16[256,128]{1,0:T(8,128)(2,1)S(1)}, bf16[256,128]{1,0:T(8,128)(2,1)S(1)}, bf16[256,128]{1,0:T(8,128)(2,1)S(1)}, bf16[256,128]{1,0:T(8,128)(2,1)S(1)}) fusion(bf16[256,256]{1,0:T(8,128)(2,1)} %param.8, bf16[256,256]{1,0:T(8,128)(2,1)} %param.9), kind=kLoop, calls=%fused_computation.15 | loop fusion | bytes 524288 | tf_op jit(solution)/shard_map/slice | solution.py:219
  1.6 0.0 copy-start
  1.6 1.9 %collective-permute-start.1 = (bf16[256,512]{1,0:T(8,128)(2,1)S(1)}, bf16[256,512]{1,0:T(8,128)(2,1)S(1)}, u32[]{:S(2)}, u32[]{:S(2)}) collective-permute-start(bf16[256,512]{1,0:T(8,128)(2,1)S(1)} %pad_maximum_fusion.refs_5_), channel_id=1, source_target_pairs={{0,1},{1,2},{2,3},{3,4},{4,5},{5,6},{6,7},{7,8},{8,9},{9,10},{10,1... | collective-permute-start | bytes 786440 | tf_op jit(solution)/shard_map/ppermute | solution.py:20
  3.6 3.4 %collective-permute-start = (bf16[256,512]{1,0:T(8,128)(2,1)S(1)}, bf16[256,512]{1,0:T(8,128)(2,1)S(1)}, u32[]{:S(2)}, u32[]{:S(2)}) collective-permute-start(bf16[256,512]{1,0:T(8,128)(2,1)S(1)} %pad_maximum_fusion.refs_5_), channel_id=1, source_target_pairs={{0,2},{1,3},{2,4},{3,5},{4,6},{5,7},{6,8},{7,9},{8,10},{9,11},{10,... | collective-permute-start | bytes 786440 | tf_op jit(solution)/shard_map/ppermute | solution.py:20
  7.0 0.7 %copy.16 = s32[16,1]{1,0:T(8,128)S(1)} copy(s32[16,1]{0,1:T(1,128)} %bitcast.1) | data formatting | bytes 128 | tf_op jit(solution)/shard_map/reshape.26
  7.8 0.1 reduce
  7.9 0.1 convert_reduce_fusion
  8.0 0.8 %fusion.2.refs_4_ = f32[256,256]{1,0:T(8,128)} fusion(s32[256]{0:T(256)S(1)} %slice.32), kind=kLoop, calls=%fused_computation.7 | loop fusion | flops 262144 | bytes 263168 | tf_op jit(solution)/shard_map/jit(_where)/select_n | solution.py:212
  8.8 0.0 copy-done
  8.8 6.8 %shard_map.94 = (f32[256,2048]{1,0:T(8,128)}, f32[256,512]{1,0:T(8,128)}) custom-call(bf16[256,4096]{1,0:T(8,128)(2,1)} %refs_0_.7, bf16[256,4096]{1,0:T(8,128)(2,1)} %refs_1_.7, bf16[256,4096]{1,0:T(8,128)(2,1)} %refs_2_.7, f32[32,256]{1,0:T(8,128)} %refs_3_.7, f32[256,256]{1,0:T(8,128)} %fusion.2.refs_4_, bf16[256,512]{1,0:T(8,128)(2,1)} %copy-done), custom_call_target="tpu_custom_call" | custom-call | tf_op jit(solution)/shard_map/pallas_call | solution.py:184
  15.6 0.9 %compare_select_fusion.refs_4_ = f32[512,256]{1,0:T(8,128)} fusion(s32[256]{0:T(256)S(1)} %slice.32, s32[512]{0:T(512)S(1)} %slice.37), kind=kLoop, calls=%fused_computation.1 | loop fusion | flops 262144 | bytes 527360 | tf_op jit(solution)/shard_map/jit(_where)/select_n | solution.py:214
  16.6 0.0 collective-permute-done.1.refs_6_
  16.6 0.0 copy-start.1
  16.6 0.0 collective-permute-done.refs_5_
  16.6 0.0 copy-start.2
  16.6 0.7 %copy-done.1 = bf16[256,512]{1,0:T(8,128)(2,1)} copy-done((bf16[256,512]{1,0:T(8,128)(2,1)}, bf16[256,512]{1,0:T(8,128)(2,1)S(1)}, u32[]{:S(2)}) %copy-start.1) | copy-done | bytes 262168
  17.3 0.1 copy-done.2
  17.4 9.8 %shard_map.95 = (bf16[256,4096]{1,0:T(8,128)(2,1)}, bf16[256,512]{1,0:T(8,128)(2,1)}, bf16[256,512]{1,0:T(8,128)(2,1)}) custom-call(bf16[256,4096]{1,0:T(8,128)(2,1)} %refs_0_.7, bf16[256,4096]{1,0:T(8,128)(2,1)} %refs_1_.7, bf16[256,4096]{1,0:T(8,128)(2,1)} %refs_2_.7, f32[32,256]{1,0:T(8,128)} %refs_3_.7, f32[512,256]{1,0:T(8,128)} %compare_select_fusion.refs_4_, ...), custom_call_target="tpu_custom_call" | custom-call | tf_op jit(solution)/shard_map/pallas_call | solution.py:184
  27.2 9.7 %shard_map.96 = (f32[256,2048]{1,0:T(8,128)}, bf16[256,512]{1,0:T(8,128)(2,1)}, bf16[256,512]{1,0:T(8,128)(2,1)}) custom-call(bf16[256,4096]{1,0:T(8,128)(2,1)} %refs_0_.7, bf16[256,4096]{1,0:T(8,128)(2,1)} %refs_1_.7, bf16[256,4096]{1,0:T(8,128)(2,1)} %refs_2_.7, f32[32,256]{1,0:T(8,128)} %refs_3_.7, ...), custom_call_target="tpu_custom_call", output_to_operand_aliasing={{1}: (7, {}), {2}: (8, {})} | custom-call | tf_op jit(solution)/shard_map/pallas_call | solution.py:184
  36.9 3.4 %collective-permute-start.2 = (bf16[256,512]{1,0:T(8,128)(2,1)}, bf16[256,512]{1,0:T(8,128)(2,1)S(1)}, u32[]{:S(2)}, u32[]{:S(2)}) collective-permute-start(bf16[256,512]{1,0:T(8,128)(2,1)} %get-tuple-element.21), channel_id=1, source_target_pairs={{1,0},{2,1},{3,2},{4,3},{5,4},{6,5},{7,6},{8,7},{9,8},{10,9},{11,1... | collective-permute-start | bytes 786440 | tf_op jit(solution)/shard_map/ppermute | solution.py:20
  40.3 3.3 %collective-permute-start.3 = (bf16[256,512]{1,0:T(8,128)(2,1)}, bf16[256,512]{1,0:T(8,128)(2,1)S(1)}, u32[]{:S(2)}, u32[]{:S(2)}) collective-permute-start(bf16[256,512]{1,0:T(8,128)(2,1)} %get-tuple-element.22), channel_id=1, source_target_pairs={{2,0},{3,1},{4,2},{5,3},{6,4},{7,5},{8,6},{9,7},{10,8},{11,9},{12,... | collective-permute-start | bytes 786440 | tf_op jit(solution)/shard_map/ppermute | solution.py:20
  43.6 6.9 %shard_map.97 = (bf16[256,4096]{1,0:T(8,128)(2,1)}, f32[256,512]{1,0:T(8,128)}) custom-call(bf16[256,4096]{1,0:T(8,128)(2,1)} %refs_0_.7, bf16[256,4096]{1,0:T(8,128)(2,1)} %refs_1_.7, bf16[256,4096]{1,0:T(8,128)(2,1)} %refs_2_.7, f32[32,256]{1,0:T(8,128)} %refs_3_.7, f32[256,256]{1,0:T(8,128)} %fusion.2.refs_4_, ...), custom_call_target="tpu_custom_call", output_to_operand_aliasing={{0}: (7, {}), {1}: (8, {})} | custom-call | tf_op jit(solution)/shard_map/pallas_call | solution.py:184
  50.5 0.0 collective-permute-done.2
  50.5 2.4 %collective-permute-done.3 = bf16[256,512]{1,0:T(8,128)(2,1)S(1)} collective-permute-done((bf16[256,512]{1,0:T(8,128)(2,1)}, bf16[256,512]{1,0:T(8,128)(2,1)S(1)}, u32[]{:S(2)}, u32[]{:S(2)}) %collective-permute-start.3) | collective-permute-done | bytes 262176 | tf_op jit(solution)/shard_map/ppermute | solution.py:20
  52.8 1.1 %fusion.3 = (bf16[256,512]{1,0:T(8,128)(2,1)S(1)}, f32[256,512]{1,0:T(8,128)S(1)}) fusion(bf16[256,512]{1,0:T(8,128)(2,1)S(1)} %collective-permute-done.3, f32[256,512]{1,0:T(8,128)} %get-tuple-element.20, bf16[256,512]{1,0:T(8,128)(2,1)S(1)} %collective-permute-done.2), kind=kLoop, calls=%fused_computation.12 | loop fusion | flops 655360 | bytes 1835008 | tf_op jit(solution)/shard_map/convert.3
  54.0 0.7 %pad_maximum_fusion.1 = bf16[256,256]{1,0:T(8,128)(2,1)} fusion(bf16[256,128]{1,0:T(8,128)(2,1)S(1)} %get-tuple-element.28, bf16[256,128]{1,0:T(8,128)(2,1)S(1)} %get-tuple-element.27), kind=kLoop, calls=%fused_computation.8 | loop fusion | flops 262144 | bytes 262144 | tf_op jit(solution)/shard_map/concatenate | solution.py:235
  54.7 0.7 %fusion = bf16[256,256]{1,0:T(8,128)(2,1)} fusion(f32[256,128]{1,0:T(8,128)S(1)} %get-tuple-element.26, f32[256,128]{1,0:T(8,128)S(1)} %get-tuple-element.25), kind=kLoop, calls=%fused_computation.4 | loop fusion | flops 196608 | bytes 393216 | tf_op jit(solution)/shard_map/convert_element_type | solution.py:239
  (8 shorter events, 0.1 us)
Async XLA Ops:
  1.6 7.2 %copy-start = (bf16[256,512]{1,0:T(8,128)(2,1)}, bf16[256,512]{1,0:T(8,128)(2,1)S(1)}, u32[]{:S(2)}) copy-start(bf16[256,512]{1,0:T(8,128)(2,1)S(1)} %pad_maximum_fusion.refs_5_) | copy-start | bytes 786436
  1.6 14.9 %collective-permute-start.1 = (bf16[256,512]{1,0:T(8,128)(2,1)S(1)}, bf16[256,512]{1,0:T(8,128)(2,1)S(1)}, u32[]{:S(2)}, u32[]{:S(2)}) collective-permute-start(bf16[256,512]{1,0:T(8,128)(2,1)S(1)} %pad_maximum_fusion.refs_5_), channel_id=1, source_target_pairs={{0,1},{1,2},{2,3},{3,4},{4,5},{5,6},{6,7},{7,8},{8,9},{9,10},{10,1... | collective-permute-start | bytes 786440 | tf_op jit(solution)/shard_map/ppermute | solution.py:20
  3.6 13.0 %collective-permute-start = (bf16[256,512]{1,0:T(8,128)(2,1)S(1)}, bf16[256,512]{1,0:T(8,128)(2,1)S(1)}, u32[]{:S(2)}, u32[]{:S(2)}) collective-permute-start(bf16[256,512]{1,0:T(8,128)(2,1)S(1)} %pad_maximum_fusion.refs_5_), channel_id=1, source_target_pairs={{0,2},{1,3},{2,4},{3,5},{4,6},{5,7},{6,8},{7,9},{8,10},{9,11},{10,... | collective-permute-start | bytes 786440 | tf_op jit(solution)/shard_map/ppermute | solution.py:20
  16.6 0.7 %copy-start.1 = (bf16[256,512]{1,0:T(8,128)(2,1)}, bf16[256,512]{1,0:T(8,128)(2,1)S(1)}, u32[]{:S(2)}) copy-start(bf16[256,512]{1,0:T(8,128)(2,1)S(1)} %collective-permute-done.1.refs_6_) | copy-start | bytes 786436
  16.6 0.8 %copy-start.2 = (bf16[256,512]{1,0:T(8,128)(2,1)}, bf16[256,512]{1,0:T(8,128)(2,1)S(1)}, u32[]{:S(2)}) copy-start(bf16[256,512]{1,0:T(8,128)(2,1)S(1)} %collective-permute-done.refs_5_) | copy-start | bytes 786436
  36.9 13.6 %collective-permute-start.2 = (bf16[256,512]{1,0:T(8,128)(2,1)}, bf16[256,512]{1,0:T(8,128)(2,1)S(1)}, u32[]{:S(2)}, u32[]{:S(2)}) collective-permute-start(bf16[256,512]{1,0:T(8,128)(2,1)} %get-tuple-element.21), channel_id=1, source_target_pairs={{1,0},{2,1},{3,2},{4,3},{5,4},{6,5},{7,6},{8,7},{9,8},{10,9},{11,1... | collective-permute-start | bytes 786440 | tf_op jit(solution)/shard_map/ppermute | solution.py:20
  40.3 12.6 %collective-permute-start.3 = (bf16[256,512]{1,0:T(8,128)(2,1)}, bf16[256,512]{1,0:T(8,128)(2,1)S(1)}, u32[]{:S(2)}, u32[]{:S(2)}) collective-permute-start(bf16[256,512]{1,0:T(8,128)(2,1)} %get-tuple-element.22), channel_id=1, source_target_pairs={{2,0},{3,1},{4,2},{5,3},{6,4},{7,5},{8,6},{9,7},{10,8},{11,9},{12,... | collective-permute-start | bytes 786440 | tf_op jit(solution)/shard_map/ppermute | solution.py:20

commit v3 on v2

--- a/solution.py
+++ b/solution.py
@@ -20,7 +20,7 @@
     return lax.ppermute(block, axis, route)
 
 
-def make_kernel(tok, reach, remote, dq_in, dq_final, n_alias):
+def make_kernel(tok, reach, remote, dq_in, dq_final, n_alias, delta_in):
     hb = HEADS_PER_STEP
     pieces = list(range(reach)) if remote else [reach]
     tiles_per_piece = tok // KEY_TILE
@@ -34,6 +34,7 @@
         rest = rest[n_alias:]
         dq_ref = rest.pop(0)
         dkv_refs = [rest.pop(0) for _ in pieces]
+        dl_out = None if delta_in else rest.pop(0)
         qs_scr, dos_scr, dqt_scr, kt_scr, acc_scr = rest[-5:]
         b = pl.program_id(0)
         nb = pl.num_programs(0)
@@ -50,8 +51,13 @@
             cols = slice(i * HD, (i + 1) * HD)
             qs_scr[i * tok:(i + 1) * tok, :] = q_ref[:, cols]
             dos_scr[i * tok:(i + 1) * tok, :] = do_ref[:, cols]
-            prod = do_ref[:, cols].astype(jnp.float32) * o_ref[:, cols].astype(jnp.float32)
-            delta_rows.append(jnp.sum(prod.T, axis=0, keepdims=True))
+            if delta_in:
+                delta_rows.append(o_ref[i:i + 1, :])
+            else:
+                prod = do_ref[:, cols].astype(jnp.float32) * o_ref[:, cols].astype(jnp.float32)
+                row = jnp.sum(prod.T, axis=0, keepdims=True)
+                dl_out[i:i + 1, :] = row
+                delta_rows.append(row)
         dl_row = jnp.concatenate(delta_rows, axis=1)
         lse_row = jnp.concatenate([lse_ref[i:i + 1, :] for i in range(hb)], axis=1)
         dqt_scr[...] = jnp.zeros_like(dqt_scr)
@@ -101,7 +107,7 @@
 
 
 def grads_call(group, remote, flags, queries, out_grad, outputs, lse, bias, kv_pieces,
-               reach, dq_part=None, dq_alias=None, dkv_alias=None):
+               reach, dq_part=None, dq_alias=None, dkv_alias=None, delta=None):
     tok, width = queries.shape
     n_heads = width // HD
     kvh = kv_pieces[0].shape[1] // (2 * HD)
@@ -121,6 +127,9 @@
     def local_block(b, *f):
         return (0, b)
 
+    def local_rows(b, *f):
+        return (b, 0)
+
     def bias_block(b, *f):
         return (0, 0)
 
@@ -130,11 +139,12 @@
     in_specs = [
         pl.BlockSpec((tok, hb * HD), head_block),
         pl.BlockSpec((tok, hb * HD), head_block),
-        pl.BlockSpec((tok, hb * HD), head_block),
+        pl.BlockSpec((tok, hb * HD), head_block) if delta is None
+        else pl.BlockSpec((hb, tok), local_rows),
         pl.BlockSpec((hb, tok), lse_block),
         pl.BlockSpec((n_pieces * tok, tok), bias_block),
     ] + [pl.BlockSpec((tok, 2 * HD), kv_block) for _ in pieces]
-    args = [queries, out_grad, outputs, lse, bias] + [kv_pieces[reach - p] for p in pieces]
+    args = [queries, out_grad, outputs if delta is None else delta, lse, bias] + [kv_pieces[reach - p] for p in pieces]
     if dq_part is not None:
         in_specs.append(pl.BlockSpec((tok, hb * HD), local_block))
         args.append(dq_part)
@@ -149,7 +159,11 @@
             in_specs.append(pl.BlockSpec(memory_space=pl.ANY))
             args.append(piece_arr)
 
-    kernel = make_kernel(tok, reach, remote, dq_part is not None, dq_final, len(aliases))
+    kernel = make_kernel(tok, reach, remote, dq_part is not None, dq_final, len(aliases),
+                         delta is not None)
+    extra_shape = [] if delta is not None else [
+        jax.ShapeDtypeStruct((heads_per_group, tok), jnp.float32)]
+    extra_spec = [] if delta is not None else [pl.BlockSpec((hb, tok), local_rows)]
     if dq_final:
         dq_shape = jax.ShapeDtypeStruct((tok, width), jnp.bfloat16)
         dq_spec = pl.BlockSpec((tok, hb * HD), head_block)
@@ -172,7 +186,7 @@
         num_scalar_prefetch=0,
         grid=(nb,),
         in_specs=in_specs,
-        out_specs=[dq_spec] + [dkv_spec] * n_pieces,
+        out_specs=[dq_spec] + [dkv_spec] * n_pieces + extra_spec,
         scratch_shapes=[
             pltpu.VMEM((hb * tok, HD), jnp.bfloat16),
             pltpu.VMEM((hb * tok, HD), jnp.bfloat16),
@@ -184,11 +198,11 @@
     outs = pl.pallas_call(
         kernel,
         grid_spec=grid_spec,
-        out_shape=[dq_shape] + [dkv_shape] * n_pieces,
+        out_shape=[dq_shape] + [dkv_shape] * n_pieces + extra_shape,
         input_output_aliases=aliases,
         compiler_params=pltpu.CompilerParams(dimension_semantics=("arbitrary",)),
     )(*args)
-    return outs[0], outs[1:]
+    return outs[0], outs[1:1 + n_pieces], (outs[-1] if delta is None else delta)
 
 
 def per_device(queries, keys, values, outputs, out_grad, logsumexp, doc_lengths):
@@ -221,12 +235,12 @@
     own = (None, queries, out_grad, outputs, logsumexp, bias_own, kv_pieces, reach)
     rem = (None, queries, out_grad, outputs, logsumexp, bias_rem, kv_pieces, reach)
 
-    dq_part0, (dkv_own0,) = grads_call(0, False, *own)
-    dq, dkv_rem = grads_call(0, True, *rem, dq_part=dq_part0)
-    dq_part1, dkv_rem = grads_call(1, True, *rem, dkv_alias=dkv_rem)
+    dq_part0, (dkv_own0,), delta0 = grads_call(0, False, *own)
+    dq, dkv_rem, _ = grads_call(0, True, *rem, dq_part=dq_part0, delta=delta0)
+    dq_part1, dkv_rem, delta1 = grads_call(1, True, *rem, dkv_alias=dkv_rem)
     returned = [shifted(dkv_rem[reach - hop], "seq", -hop) for hop in range(1, reach + 1)]
-    dq, (total,) = grads_call(1, False, *own, dq_part=dq_part1, dq_alias=dq,
-                              dkv_alias=[dkv_own0])
+    dq, (total,), _ = grads_call(1, False, *own, dq_part=dq_part1, dq_alias=dq,
+                                 dkv_alias=[dkv_own0], delta=delta1)
 
     for r in returned:
         total = total + r.astype(jnp.float32)

time: 56.3 us -> 56.1 us (level)
  transfers between devices with their start and end apart: 4 -> 4, of which waited for: 1 -> 1; matrix products, arithmetic and copies ran while one was open for 5% -> 5% of each run, Pallas kernels for 25% -> 24%
where the time goes in v3:
time: 56.1 us; the launch traced here: 55.2 us
  Pallas kernels  32.8 us (58%)
  starting transfers between devices  12 us (21%)
  other arithmetic  4.53 us (8%)
  waiting for transfers between devices  2.55 us (5%)
  local copies, waits for them, and re-layouts  2.52 us (4%)
  between operations  0.77 us (1%)
    pallas_call x4, Pallas kernels, grads_call(): pl.pallas_call(kernel, grid_spec=grid_spec, out_shape=[dq_shape] + [dkv_s...  32.8 us
    ppermute x4, starting transfers between devices, shifted(): return lax.ppermute(block, axis, route)  12 us
    ppermute x4, waiting for transfers between devices, shifted(): return lax.ppermute(block, axis, route)  2.55 us
    another operation x3, other arithmetic  1.3 us
  transfers between devices with their start and end apart: 4, of which 1 were waited for; matrix products, arithmetic and copies ran while one was open for 5% of the time, Pallas kernels for 24%

profile of v3, /device:TPU:12, one launch (start us, length us, event | category | flops | bytes accessed | tf_op | source)
XLA Modules:
  0.0 55.2 jit_solution(10173535684528511211)
XLA Ops:
  0.6 1.0 %fusion.6 = (bf16[256,128]{1,0:T(8,128)(2,1)S(1)}, bf16[256,128]{1,0:T(8,128)(2,1)S(1)}, bf16[256,128]{1,0:T(8,128)(2,1)S(1)}, bf16[256,128]{1,0:T(8,128)(2,1)S(1)}) fusion(bf16[256,256]{1,0:T(8,128)(2,1)} %param.8, bf16[256,256]{1,0:T(8,128)(2,1)} %param.9), kind=kLoop, calls=%fused_computation.15 | loop fusion | bytes 524288 | tf_op jit(solution)/shard_map/slice | solution.py:233
  1.6 0.0 copy-start
  1.6 1.9 %collective-permute-start.1 = (bf16[256,512]{1,0:T(8,128)(2,1)S(1)}, bf16[256,512]{1,0:T(8,128)(2,1)S(1)}, u32[]{:S(2)}, u32[]{:S(2)}) collective-permute-start(bf16[256,512]{1,0:T(8,128)(2,1)S(1)} %pad_maximum_fusion.refs_5_), channel_id=1, source_target_pairs={{0,1},{1,2},{2,3},{3,4},{4,5},{5,6},{6,7},{7,8},{8,9},{9,10},{10,1... | collective-permute-start | bytes 786440 | tf_op jit(solution)/shard_map/ppermute | solution.py:20
  3.6 3.4 %collective-permute-start = (bf16[256,512]{1,0:T(8,128)(2,1)S(1)}, bf16[256,512]{1,0:T(8,128)(2,1)S(1)}, u32[]{:S(2)}, u32[]{:S(2)}) collective-permute-start(bf16[256,512]{1,0:T(8,128)(2,1)S(1)} %pad_maximum_fusion.refs_5_), channel_id=1, source_target_pairs={{0,2},{1,3},{2,4},{3,5},{4,6},{5,7},{6,8},{7,9},{8,10},{9,11},{10,... | collective-permute-start | bytes 786440 | tf_op jit(solution)/shard_map/ppermute | solution.py:20
  7.0 0.7 %copy.16 = s32[16,1]{1,0:T(8,128)S(1)} copy(s32[16,1]{0,1:T(1,128)} %bitcast.1) | data formatting | bytes 128 | tf_op jit(solution)/shard_map/reshape.26
  7.8 0.1 reduce
  7.9 0.1 convert_reduce_fusion
  8.0 0.8 %fusion.2.refs_4_ = f32[256,256]{1,0:T(8,128)} fusion(s32[256]{0:T(256)S(1)} %slice.33), kind=kLoop, calls=%fused_computation.7 | loop fusion | flops 262144 | bytes 263168 | tf_op jit(solution)/shard_map/jit(_where)/select_n | solution.py:226
  8.8 0.0 copy-done
  8.8 6.8 %shard_map.94 = (f32[256,2048]{1,0:T(8,128)}, f32[256,512]{1,0:T(8,128)}, f32[16,256]{1,0:T(8,128)}) custom-call(bf16[256,4096]{1,0:T(8,128)(2,1)} %refs_0_.7, bf16[256,4096]{1,0:T(8,128)(2,1)} %refs_1_.7, bf16[256,4096]{1,0:T(8,128)(2,1)} %refs_2_.3, f32[32,256]{1,0:T(8,128)} %refs_3_.7, f32[256,256]{1,0:T(8,128)} %fusion.2.refs_4_, bf16[256,512]{1,0:T(8,128)(2,1)} %copy-done), custom_call_target="tpu_custom_call" | custom-call | tf_op jit(solution)/shard_map/pallas_call | solution.py:198
  15.6 0.9 %compare_select_fusion.refs_4_ = f32[512,256]{1,0:T(8,128)} fusion(s32[256]{0:T(256)S(1)} %slice.33, s32[512]{0:T(512)S(1)} %slice.32), kind=kLoop, calls=%fused_computation.1 | loop fusion | flops 262144 | bytes 527360 | tf_op jit(solution)/shard_map/jit(_where)/select_n | solution.py:228
  16.6 0.0 collective-permute-done.1.refs_6_
  16.6 0.0 copy-start.1
  16.6 0.0 collective-permute-done.refs_5_
  16.6 0.0 copy-start.2
  16.6 0.7 %copy-done.1 = bf16[256,512]{1,0:T(8,128)(2,1)} copy-done((bf16[256,512]{1,0:T(8,128)(2,1)}, bf16[256,512]{1,0:T(8,128)(2,1)S(1)}, u32[]{:S(2)}) %copy-start.1) | copy-done | bytes 262168
  17.3 0.1 copy-done.2
  17.4 9.6 %shard_map.95 = (bf16[256,4096]{1,0:T(8,128)(2,1)}, bf16[256,512]{1,0:T(8,128)(2,1)}, bf16[256,512]{1,0:T(8,128)(2,1)}) custom-call(bf16[256,4096]{1,0:T(8,128)(2,1)} %refs_0_.7, bf16[256,4096]{1,0:T(8,128)(2,1)} %refs_1_.7, f32[16,256]{1,0:T(8,128)} %get-tuple-element.15.refs_2_, f32[32,256]{1,0:T(8,128)} %refs_3_.7, ...), custom_call_target="tpu_custom_call" | custom-call | tf_op jit(solution)/shard_map/pallas_call | solution.py:198
  27.0 9.7 %shard_map.96 = (f32[256,2048]{1,0:T(8,128)}, bf16[256,512]{1,0:T(8,128)(2,1)}, bf16[256,512]{1,0:T(8,128)(2,1)}, f32[16,256]{1,0:T(8,128)}) custom-call(bf16[256,4096]{1,0:T(8,128)(2,1)} %refs_0_.7, bf16[256,4096]{1,0:T(8,128)(2,1)} %refs_1_.7, bf16[256,4096]{1,0:T(8,128)(2,1)} %refs_2_.3, ...), custom_call_target="tpu_custom_call", output_to_operand_aliasing={{1}: (7, {}), {2}: (8, {})} | custom-call | tf_op jit(solution)/shard_map/pallas_call | solution.py:198
  36.7 3.4 %collective-permute-start.2 = (bf16[256,512]{1,0:T(8,128)(2,1)}, bf16[256,512]{1,0:T(8,128)(2,1)S(1)}, u32[]{:S(2)}, u32[]{:S(2)}) collective-permute-start(bf16[256,512]{1,0:T(8,128)(2,1)} %get-tuple-element.25), channel_id=1, source_target_pairs={{1,0},{2,1},{3,2},{4,3},{5,4},{6,5},{7,6},{8,7},{9,8},{10,9},{11,1... | collective-permute-start | bytes 786440 | tf_op jit(solution)/shard_map/ppermute | solution.py:20
  40.1 3.3 %collective-permute-start.3 = (bf16[256,512]{1,0:T(8,128)(2,1)}, bf16[256,512]{1,0:T(8,128)(2,1)S(1)}, u32[]{:S(2)}, u32[]{:S(2)}) collective-permute-start(bf16[256,512]{1,0:T(8,128)(2,1)} %get-tuple-element.26), channel_id=1, source_target_pairs={{2,0},{3,1},{4,2},{5,3},{6,4},{7,5},{8,6},{9,7},{10,8},{11,9},{12,... | collective-permute-start | bytes 786440 | tf_op jit(solution)/shard_map/ppermute | solution.py:20
  43.4 6.7 %shard_map.97 = (bf16[256,4096]{1,0:T(8,128)(2,1)}, f32[256,512]{1,0:T(8,128)}) custom-call(bf16[256,4096]{1,0:T(8,128)(2,1)} %refs_0_.7, bf16[256,4096]{1,0:T(8,128)(2,1)} %refs_1_.7, f32[16,256]{1,0:T(8,128)} %get-tuple-element.19.refs_2_, f32[32,256]{1,0:T(8,128)} %refs_3_.7, ...), custom_call_target="tpu_custom_call", output_to_operand_aliasing={{0}: (7, {}), {1}: (8, {})} | custom-call | tf_op jit(solution)/shard_map/pallas_call | solution.py:198
  50.1 0.0 collective-permute-done.2
  50.1 2.5 %collective-permute-done.3 = bf16[256,512]{1,0:T(8,128)(2,1)S(1)} collective-permute-done((bf16[256,512]{1,0:T(8,128)(2,1)}, bf16[256,512]{1,0:T(8,128)(2,1)S(1)}, u32[]{:S(2)}, u32[]{:S(2)}) %collective-permute-start.3) | collective-permute-done | bytes 262176 | tf_op jit(solution)/shard_map/ppermute | solution.py:20
  52.7 1.1 %fusion.3 = (bf16[256,512]{1,0:T(8,128)(2,1)S(1)}, f32[256,512]{1,0:T(8,128)S(1)}) fusion(bf16[256,512]{1,0:T(8,128)(2,1)S(1)} %collective-permute-done.3, f32[256,512]{1,0:T(8,128)} %get-tuple-element.24, bf16[256,512]{1,0:T(8,128)(2,1)S(1)} %collective-permute-done.2), kind=kLoop, calls=%fused_computation.12 | loop fusion | flops 655360 | bytes 1835008 | tf_op jit(solution)/shard_map/convert.3
  53.9 0.7 %pad_maximum_fusion.1 = bf16[256,256]{1,0:T(8,128)(2,1)} fusion(bf16[256,128]{1,0:T(8,128)(2,1)S(1)} %get-tuple-element.32, bf16[256,128]{1,0:T(8,128)(2,1)S(1)} %get-tuple-element.31), kind=kLoop, calls=%fused_computation.8 | loop fusion | flops 262144 | bytes 262144 | tf_op jit(solution)/shard_map/concatenate | solution.py:249
  54.5 0.7 %fusion = bf16[256,256]{1,0:T(8,128)(2,1)} fusion(f32[256,128]{1,0:T(8,128)S(1)} %get-tuple-element.30, f32[256,128]{1,0:T(8,128)S(1)} %get-tuple-element.29), kind=kLoop, calls=%fused_computation.4 | loop fusion | flops 196608 | bytes 393216 | tf_op jit(solution)/shard_map/convert_element_type | solution.py:253
  (8 shorter events, 0.1 us)
Async XLA Ops:
  1.6 7.2 %copy-start = (bf16[256,512]{1,0:T(8,128)(2,1)}, bf16[256,512]{1,0:T(8,128)(2,1)S(1)}, u32[]{:S(2)}) copy-start(bf16[256,512]{1,0:T(8,128)(2,1)S(1)} %pad_maximum_fusion.refs_5_) | copy-start | bytes 786436
  1.6 15.0 %collective-permute-start.1 = (bf16[256,512]{1,0:T(8,128)(2,1)S(1)}, bf16[256,512]{1,0:T(8,128)(2,1)S(1)}, u32[]{:S(2)}, u32[]{:S(2)}) collective-permute-start(bf16[256,512]{1,0:T(8,128)(2,1)S(1)} %pad_maximum_fusion.refs_5_), channel_id=1, source_target_pairs={{0,1},{1,2},{2,3},{3,4},{4,5},{5,6},{6,7},{7,8},{8,9},{9,10},{10,1... | collective-permute-start | bytes 786440 | tf_op jit(solution)/shard_map/ppermute | solution.py:20
  3.6 13.0 %collective-permute-start = (bf16[256,512]{1,0:T(8,128)(2,1)S(1)}, bf16[256,512]{1,0:T(8,128)(2,1)S(1)}, u32[]{:S(2)}, u32[]{:S(2)}) collective-permute-start(bf16[256,512]{1,0:T(8,128)(2,1)S(1)} %pad_maximum_fusion.refs_5_), channel_id=1, source_target_pairs={{0,2},{1,3},{2,4},{3,5},{4,6},{5,7},{6,8},{7,9},{8,10},{9,11},{10,... | collective-permute-start | bytes 786440 | tf_op jit(solution)/shard_map/ppermute | solution.py:20
  16.6 0.7 %copy-start.1 = (bf16[256,512]{1,0:T(8,128)(2,1)}, bf16[256,512]{1,0:T(8,128)(2,1)S(1)}, u32[]{:S(2)}) copy-start(bf16[256,512]{1,0:T(8,128)(2,1)S(1)} %collective-permute-done.1.refs_6_) | copy-start | bytes 786436
  16.6 0.8 %copy-start.2 = (bf16[256,512]{1,0:T(8,128)(2,1)}, bf16[256,512]{1,0:T(8,128)(2,1)S(1)}, u32[]{:S(2)}) copy-start(bf16[256,512]{1,0:T(8,128)(2,1)S(1)} %collective-permute-done.refs_5_) | copy-start | bytes 786436
  36.7 13.4 %collective-permute-start.2 = (bf16[256,512]{1,0:T(8,128)(2,1)}, bf16[256,512]{1,0:T(8,128)(2,1)S(1)}, u32[]{:S(2)}, u32[]{:S(2)}) collective-permute-start(bf16[256,512]{1,0:T(8,128)(2,1)} %get-tuple-element.25), channel_id=1, source_target_pairs={{1,0},{2,1},{3,2},{4,3},{5,4},{6,5},{7,6},{8,7},{9,8},{10,9},{11,1... | collective-permute-start | bytes 786440 | tf_op jit(solution)/shard_map/ppermute | solution.py:20
  40.1 12.6 %collective-permute-start.3 = (bf16[256,512]{1,0:T(8,128)(2,1)}, bf16[256,512]{1,0:T(8,128)(2,1)S(1)}, u32[]{:S(2)}, u32[]{:S(2)}) collective-permute-start(bf16[256,512]{1,0:T(8,128)(2,1)} %get-tuple-element.26), channel_id=1, source_target_pairs={{2,0},{3,1},{4,2},{5,3},{6,4},{7,5},{8,6},{9,7},{10,8},{11,9},{12,... | collective-permute-start | bytes 786440 | tf_op jit(solution)/shard_map/ppermute | solution.py:20

commit v4 on v3

--- a/solution.py
+++ b/solution.py
@@ -62,9 +62,29 @@
         lse_row = jnp.concatenate([lse_ref[i:i + 1, :] for i in range(hb)], axis=1)
         dqt_scr[...] = jnp.zeros_like(dqt_scr)
 
+        if tiles_per_piece == 1 and len(pieces) > 1:
+            k = jnp.concatenate([kv[:, :HD] for kv in kv_refs], axis=0)
+            v = jnp.concatenate([kv[:, HD:] for kv in kv_refs], axis=0)
+            qs = qs_scr[...]
+            dos = dos_scr[...]
+            st = lax.dot_general(k, qs, NT_DIMS, preferred_element_type=jnp.float32)
+            bias = bias_ref[...]
+            p = jnp.exp(st * scale - lse_row + jnp.concatenate([bias] * hb, axis=1))
+            dv = jnp.dot(p.astype(jnp.bfloat16), dos, preferred_element_type=jnp.float32)
+            dpt = lax.dot_general(v, dos, NT_DIMS, preferred_element_type=jnp.float32)
+            ds = (p * (dpt - dl_row)).astype(jnp.bfloat16)
+            dk = jnp.dot(ds, qs, preferred_element_type=jnp.float32)
+            for n in range(len(pieces)):
+                acc_scr[n, :, :HD] += dk[n * tok:(n + 1) * tok]
+                acc_scr[n, :, HD:] += dv[n * tok:(n + 1) * tok]
+            dqt_scr[...] += jnp.dot(kt_scr[...], ds, preferred_element_type=jnp.float32)
+            tiles_per_piece_loop = 0
+        else:
+            tiles_per_piece_loop = tiles_per_piece
+
         for n, piece in enumerate(pieces):
             kv = kv_refs[n]
-            for t in range(tiles_per_piece):
+            for t in range(tiles_per_piece_loop):
                 j = piece * tiles_per_piece + t
                 rows = slice(t * KEY_TILE, (t + 1) * KEY_TILE)
                 loc_rows = slice(n * tok + t * KEY_TILE, n * tok + (t + 1) * KEY_TILE)

time: 56.1 us -> 55.7 us (level)
  transfers between devices with their start and end apart: 4 -> 4, of which waited for: 1 -> 1; matrix products, arithmetic and copies ran while one was open for 5% -> 5% of each run, Pallas kernels for 24% -> 25%
where the time goes in v4:
time: 55.7 us; the launch traced here: 54.8 us
  Pallas kernels  32.4 us (58%)
  starting transfers between devices  12 us (22%)
  other arithmetic  4.53 us (8%)
  waiting for transfers between devices  2.56 us (5%)
  local copies, waits for them, and re-layouts  2.52 us (5%)
  between operations  0.77 us (1%)
    pallas_call x4, Pallas kernels, grads_call(): pl.pallas_call(kernel, grid_spec=grid_spec, out_shape=[dq_shape] + [dkv_s...  32.4 us
    ppermute x4, starting transfers between devices, shifted(): return lax.ppermute(block, axis, route)  12 us
    ppermute x4, waiting for transfers between devices, shifted(): return lax.ppermute(block, axis, route)  2.56 us
    another operation x3, other arithmetic  1.3 us
  transfers between devices with their start and end apart: 4, of which 1 were waited for; matrix products, arithmetic and copies ran while one was open for 5% of the time, Pallas kernels for 25%

profile of v4, /device:TPU:12, one launch (start us, length us, event | category | flops | bytes accessed | tf_op | source)
XLA Modules:
  0.0 54.8 jit_solution(4955446039420121566)
XLA Ops:
  0.6 1.0 %fusion.6 = (bf16[256,128]{1,0:T(8,128)(2,1)S(1)}, bf16[256,128]{1,0:T(8,128)(2,1)S(1)}, bf16[256,128]{1,0:T(8,128)(2,1)S(1)}, bf16[256,128]{1,0:T(8,128)(2,1)S(1)}) fusion(bf16[256,256]{1,0:T(8,128)(2,1)} %param.8, bf16[256,256]{1,0:T(8,128)(2,1)} %param.9), kind=kLoop, calls=%fused_computation.15 | loop fusion | bytes 524288 | tf_op jit(solution)/shard_map/slice | solution.py:253
  1.6 0.0 copy-start
  1.6 1.9 %collective-permute-start.1 = (bf16[256,512]{1,0:T(8,128)(2,1)S(1)}, bf16[256,512]{1,0:T(8,128)(2,1)S(1)}, u32[]{:S(2)}, u32[]{:S(2)}) collective-permute-start(bf16[256,512]{1,0:T(8,128)(2,1)S(1)} %pad_maximum_fusion.refs_5_), channel_id=1, source_target_pairs={{0,1},{1,2},{2,3},{3,4},{4,5},{5,6},{6,7},{7,8},{8,9},{9,10},{10,1... | collective-permute-start | bytes 786440 | tf_op jit(solution)/shard_map/ppermute | solution.py:20
  3.6 3.4 %collective-permute-start = (bf16[256,512]{1,0:T(8,128)(2,1)S(1)}, bf16[256,512]{1,0:T(8,128)(2,1)S(1)}, u32[]{:S(2)}, u32[]{:S(2)}) collective-permute-start(bf16[256,512]{1,0:T(8,128)(2,1)S(1)} %pad_maximum_fusion.refs_5_), channel_id=1, source_target_pairs={{0,2},{1,3},{2,4},{3,5},{4,6},{5,7},{6,8},{7,9},{8,10},{9,11},{10,... | collective-permute-start | bytes 786440 | tf_op jit(solution)/shard_map/ppermute | solution.py:20
  7.0 0.7 %copy.16 = s32[16,1]{1,0:T(8,128)S(1)} copy(s32[16,1]{0,1:T(1,128)} %bitcast.1) | data formatting | bytes 128 | tf_op jit(solution)/shard_map/reshape.26
  7.8 0.1 reduce
  7.9 0.1 convert_reduce_fusion
  8.0 0.8 %fusion.2.refs_4_ = f32[256,256]{1,0:T(8,128)} fusion(s32[256]{0:T(256)S(1)} %slice.33), kind=kLoop, calls=%fused_computation.7 | loop fusion | flops 262144 | bytes 263168 | tf_op jit(solution)/shard_map/jit(_where)/select_n | solution.py:246
  8.8 0.0 copy-done
  8.8 6.8 %shard_map.94 = (f32[256,2048]{1,0:T(8,128)}, f32[256,512]{1,0:T(8,128)}, f32[16,256]{1,0:T(8,128)}) custom-call(bf16[256,4096]{1,0:T(8,128)(2,1)} %refs_0_.7, bf16[256,4096]{1,0:T(8,128)(2,1)} %refs_1_.7, bf16[256,4096]{1,0:T(8,128)(2,1)} %refs_2_.3, f32[32,256]{1,0:T(8,128)} %refs_3_.7, f32[256,256]{1,0:T(8,128)} %fusion.2.refs_4_, bf16[256,512]{1,0:T(8,128)(2,1)} %copy-done), custom_call_target="tpu_custom_call" | custom-call | tf_op jit(solution)/shard_map/pallas_call | solution.py:218
  15.6 0.9 %compare_select_fusion.refs_4_ = f32[512,256]{1,0:T(8,128)} fusion(s32[256]{0:T(256)S(1)} %slice.33, s32[512]{0:T(512)S(1)} %slice.32), kind=kLoop, calls=%fused_computation.1 | loop fusion | flops 262144 | bytes 527360 | tf_op jit(solution)/shard_map/jit(_where)/select_n | solution.py:248
  16.6 0.0 collective-permute-done.1.refs_6_
  16.6 0.0 copy-start.1
  16.6 0.0 collective-permute-done.refs_5_
  16.6 0.0 copy-start.2
  16.6 0.7 %copy-done.1 = bf16[256,512]{1,0:T(8,128)(2,1)} copy-done((bf16[256,512]{1,0:T(8,128)(2,1)}, bf16[256,512]{1,0:T(8,128)(2,1)S(1)}, u32[]{:S(2)}) %copy-start.1) | copy-done | bytes 262168
  17.3 0.1 copy-done.2
  17.4 9.4 %shard_map.95 = (bf16[256,4096]{1,0:T(8,128)(2,1)}, bf16[256,512]{1,0:T(8,128)(2,1)}, bf16[256,512]{1,0:T(8,128)(2,1)}) custom-call(bf16[256,4096]{1,0:T(8,128)(2,1)} %refs_0_.7, bf16[256,4096]{1,0:T(8,128)(2,1)} %refs_1_.7, f32[16,256]{1,0:T(8,128)} %get-tuple-element.15.refs_2_, f32[32,256]{1,0:T(8,128)} %refs_3_.7, ...), custom_call_target="tpu_custom_call" | custom-call | tf_op jit(solution)/shard_map/pallas_call | solution.py:218
  26.8 9.6 %shard_map.96 = (f32[256,2048]{1,0:T(8,128)}, bf16[256,512]{1,0:T(8,128)(2,1)}, bf16[256,512]{1,0:T(8,128)(2,1)}, f32[16,256]{1,0:T(8,128)}) custom-call(bf16[256,4096]{1,0:T(8,128)(2,1)} %refs_0_.7, bf16[256,4096]{1,0:T(8,128)(2,1)} %refs_1_.7, bf16[256,4096]{1,0:T(8,128)(2,1)} %refs_2_.3, ...), custom_call_target="tpu_custom_call", output_to_operand_aliasing={{1}: (7, {}), {2}: (8, {})} | custom-call | tf_op jit(solution)/shard_map/pallas_call | solution.py:218
  36.3 3.4 %collective-permute-start.2 = (bf16[256,512]{1,0:T(8,128)(2,1)}, bf16[256,512]{1,0:T(8,128)(2,1)S(1)}, u32[]{:S(2)}, u32[]{:S(2)}) collective-permute-start(bf16[256,512]{1,0:T(8,128)(2,1)} %get-tuple-element.25), channel_id=1, source_target_pairs={{1,0},{2,1},{3,2},{4,3},{5,4},{6,5},{7,6},{8,7},{9,8},{10,9},{11,1... | collective-permute-start | bytes 786440 | tf_op jit(solution)/shard_map/ppermute | solution.py:20
  39.7 3.3 %collective-permute-start.3 = (bf16[256,512]{1,0:T(8,128)(2,1)}, bf16[256,512]{1,0:T(8,128)(2,1)S(1)}, u32[]{:S(2)}, u32[]{:S(2)}) collective-permute-start(bf16[256,512]{1,0:T(8,128)(2,1)} %get-tuple-element.26), channel_id=1, source_target_pairs={{2,0},{3,1},{4,2},{5,3},{6,4},{7,5},{8,6},{9,7},{10,8},{11,9},{12,... | collective-permute-start | bytes 786440 | tf_op jit(solution)/shard_map/ppermute | solution.py:20
  43.0 6.7 %shard_map.97 = (bf16[256,4096]{1,0:T(8,128)(2,1)}, f32[256,512]{1,0:T(8,128)}) custom-call(bf16[256,4096]{1,0:T(8,128)(2,1)} %refs_0_.7, bf16[256,4096]{1,0:T(8,128)(2,1)} %refs_1_.7, f32[16,256]{1,0:T(8,128)} %get-tuple-element.19.refs_2_, f32[32,256]{1,0:T(8,128)} %refs_3_.7, ...), custom_call_target="tpu_custom_call", output_to_operand_aliasing={{0}: (7, {}), {1}: (8, {})} | custom-call | tf_op jit(solution)/shard_map/pallas_call | solution.py:218
  49.7 0.0 collective-permute-done.2
  49.7 2.5 %collective-permute-done.3 = bf16[256,512]{1,0:T(8,128)(2,1)S(1)} collective-permute-done((bf16[256,512]{1,0:T(8,128)(2,1)}, bf16[256,512]{1,0:T(8,128)(2,1)S(1)}, u32[]{:S(2)}, u32[]{:S(2)}) %collective-permute-start.3) | collective-permute-done | bytes 262176 | tf_op jit(solution)/shard_map/ppermute | solution.py:20
  52.3 1.1 %fusion.3 = (bf16[256,512]{1,0:T(8,128)(2,1)S(1)}, f32[256,512]{1,0:T(8,128)S(1)}) fusion(bf16[256,512]{1,0:T(8,128)(2,1)S(1)} %collective-permute-done.3, f32[256,512]{1,0:T(8,128)} %get-tuple-element.24, bf16[256,512]{1,0:T(8,128)(2,1)S(1)} %collective-permute-done.2), kind=kLoop, calls=%fused_computation.12 | loop fusion | flops 655360 | bytes 1835008 | tf_op jit(solution)/shard_map/convert.3
  53.5 0.7 %pad_maximum_fusion.1 = bf16[256,256]{1,0:T(8,128)(2,1)} fusion(bf16[256,128]{1,0:T(8,128)(2,1)S(1)} %get-tuple-element.32, bf16[256,128]{1,0:T(8,128)(2,1)S(1)} %get-tuple-element.31), kind=kLoop, calls=%fused_computation.8 | loop fusion | flops 262144 | bytes 262144 | tf_op jit(solution)/shard_map/concatenate | solution.py:269
  54.1 0.7 %fusion = bf16[256,256]{1,0:T(8,128)(2,1)} fusion(f32[256,128]{1,0:T(8,128)S(1)} %get-tuple-element.30, f32[256,128]{1,0:T(8,128)S(1)} %get-tuple-element.29), kind=kLoop, calls=%fused_computation.4 | loop fusion | flops 196608 | bytes 393216 | tf_op jit(solution)/shard_map/convert_element_type | solution.py:273
  (8 shorter events, 0.1 us)
Async XLA Ops:
  1.6 7.2 %copy-start = (bf16[256,512]{1,0:T(8,128)(2,1)}, bf16[256,512]{1,0:T(8,128)(2,1)S(1)}, u32[]{:S(2)}) copy-start(bf16[256,512]{1,0:T(8,128)(2,1)S(1)} %pad_maximum_fusion.refs_5_) | copy-start | bytes 786436
  1.6 15.0 %collective-permute-start.1 = (bf16[256,512]{1,0:T(8,128)(2,1)S(1)}, bf16[256,512]{1,0:T(8,128)(2,1)S(1)}, u32[]{:S(2)}, u32[]{:S(2)}) collective-permute-start(bf16[256,512]{1,0:T(8,128)(2,1)S(1)} %pad_maximum_fusion.refs_5_), channel_id=1, source_target_pairs={{0,1},{1,2},{2,3},{3,4},{4,5},{5,6},{6,7},{7,8},{8,9},{9,10},{10,1... | collective-permute-start | bytes 786440 | tf_op jit(solution)/shard_map/ppermute | solution.py:20
  3.6 13.0 %collective-permute-start = (bf16[256,512]{1,0:T(8,128)(2,1)S(1)}, bf16[256,512]{1,0:T(8,128)(2,1)S(1)}, u32[]{:S(2)}, u32[]{:S(2)}) collective-permute-start(bf16[256,512]{1,0:T(8,128)(2,1)S(1)} %pad_maximum_fusion.refs_5_), channel_id=1, source_target_pairs={{0,2},{1,3},{2,4},{3,5},{4,6},{5,7},{6,8},{7,9},{8,10},{9,11},{10,... | collective-permute-start | bytes 786440 | tf_op jit(solution)/shard_map/ppermute | solution.py:20
  16.6 0.7 %copy-start.1 = (bf16[256,512]{1,0:T(8,128)(2,1)}, bf16[256,512]{1,0:T(8,128)(2,1)S(1)}, u32[]{:S(2)}) copy-start(bf16[256,512]{1,0:T(8,128)(2,1)S(1)} %collective-permute-done.1.refs_6_) | copy-start | bytes 786436
  16.6 0.8 %copy-start.2 = (bf16[256,512]{1,0:T(8,128)(2,1)}, bf16[256,512]{1,0:T(8,128)(2,1)S(1)}, u32[]{:S(2)}) copy-start(bf16[256,512]{1,0:T(8,128)(2,1)S(1)} %collective-permute-done.refs_5_) | copy-start | bytes 786436
  36.3 13.4 %collective-permute-start.2 = (bf16[256,512]{1,0:T(8,128)(2,1)}, bf16[256,512]{1,0:T(8,128)(2,1)S(1)}, u32[]{:S(2)}, u32[]{:S(2)}) collective-permute-start(bf16[256,512]{1,0:T(8,128)(2,1)} %get-tuple-element.25), channel_id=1, source_target_pairs={{1,0},{2,1},{3,2},{4,3},{5,4},{6,5},{7,6},{8,7},{9,8},{10,9},{11,1... | collective-permute-start | bytes 786440 | tf_op jit(solution)/shard_map/ppermute | solution.py:20
  39.7 12.6 %collective-permute-start.3 = (bf16[256,512]{1,0:T(8,128)(2,1)}, bf16[256,512]{1,0:T(8,128)(2,1)S(1)}, u32[]{:S(2)}, u32[]{:S(2)}) collective-permute-start(bf16[256,512]{1,0:T(8,128)(2,1)} %get-tuple-element.26), channel_id=1, source_target_pairs={{2,0},{3,1},{4,2},{5,3},{6,4},{7,5},{8,6},{9,7},{10,8},{11,9},{12,... | collective-permute-start | bytes 786440 | tf_op jit(solution)/shard_map/ppermute | solution.py:20

commit v5 on v4

--- a/solution.py
+++ b/solution.py
@@ -35,7 +35,9 @@
         dq_ref = rest.pop(0)
         dkv_refs = [rest.pop(0) for _ in pieces]
         dl_out = None if delta_in else rest.pop(0)
-        qs_scr, dos_scr, dqt_scr, kt_scr, acc_scr = rest[-5:]
+        qs_out = None if delta_in else rest.pop(0)
+        dos_out = None if delta_in else rest.pop(0)
+        _, _, dqt_scr, kt_scr, acc_scr = rest[-5:]
         b = pl.program_id(0)
         nb = pl.num_programs(0)
 
@@ -46,11 +48,16 @@
                 kt_scr[:, n * tok:(n + 1) * tok] = (
                     kv[:, :HD].astype(jnp.float32).T.astype(jnp.bfloat16))
 
+        if delta_in:
+            qs_scr, dos_scr = q_ref, do_ref
+        else:
+            qs_scr, dos_scr = qs_out, dos_out
         delta_rows = []
         for i in range(hb):
             cols = slice(i * HD, (i + 1) * HD)
-            qs_scr[i * tok:(i + 1) * tok, :] = q_ref[:, cols]
-            dos_scr[i * tok:(i + 1) * tok, :] = do_ref[:, cols]
+            if not delta_in:
+                qs_scr[i * tok:(i + 1) * tok, :] = q_ref[:, cols]
+                dos_scr[i * tok:(i + 1) * tok, :] = do_ref[:, cols]
             if delta_in:
                 delta_rows.append(o_ref[i:i + 1, :])
             else:
@@ -156,14 +163,17 @@
     def kv_block(b, *f):
         return (0, group)
 
+    stacked = pl.BlockSpec((hb * tok, HD), local_rows)
     in_specs = [
-        pl.BlockSpec((tok, hb * HD), head_block),
-        pl.BlockSpec((tok, hb * HD), head_block),
+        pl.BlockSpec((tok, hb * HD), head_block) if delta is None else stacked,
+        pl.BlockSpec((tok, hb * HD), head_block) if delta is None else stacked,
         pl.BlockSpec((tok, hb * HD), head_block) if delta is None
         else pl.BlockSpec((hb, tok), local_rows),
         pl.BlockSpec((hb, tok), lse_block),
         pl.BlockSpec((n_pieces * tok, tok), bias_block),
     ] + [pl.BlockSpec((tok, 2 * HD), kv_block) for _ in pieces]
+    if delta is not None:
+        delta, queries, out_grad = delta
     args = [queries, out_grad, outputs if delta is None else delta, lse, bias] + [kv_pieces[reach - p] for p in pieces]
     if dq_part is not None:
         in_specs.append(pl.BlockSpec((tok, hb * HD), local_block))
@@ -181,9 +191,12 @@
 
     kernel = make_kernel(tok, reach, remote, dq_part is not None, dq_final, len(aliases),
                          delta is not None)
+    stack_shape = jax.ShapeDtypeStruct((heads_per_group * tok, HD), jnp.bfloat16)
     extra_shape = [] if delta is not None else [
-        jax.ShapeDtypeStruct((heads_per_group, tok), jnp.float32)]
-    extra_spec = [] if delta is not None else [pl.BlockSpec((hb, tok), local_rows)]
+        jax.ShapeDtypeStruct((heads_per_group, tok), jnp.float32), stack_shape, stack_shape]
+    extra_spec = [] if delta is not None else [
+        pl.BlockSpec((hb, tok), local_rows), pl.BlockSpec((hb * tok, HD), local_rows),
+        pl.BlockSpec((hb * tok, HD), local_rows)]
     if dq_final:
         dq_shape = jax.ShapeDtypeStruct((tok, width), jnp.bfloat16)
         dq_spec = pl.BlockSpec((tok, hb * HD), head_block)
@@ -222,7 +235,7 @@
         input_output_aliases=aliases,
         compiler_params=pltpu.CompilerParams(dimension_semantics=("arbitrary",)),
     )(*args)
-    return outs[0], outs[1:1 + n_pieces], (outs[-1] if delta is None else delta)
+    return outs[0], outs[1:1 + n_pieces], (tuple(outs[-3:]) if delta is None else None)
 
 
 def per_device(queries, keys, values, outputs, out_grad, logsumexp, doc_lengths):

time: 55.7 us -> 55.9 us (level)
  no operation moved by 1% of the time
where the time goes in v5:
time: 55.9 us; the launch traced here: 55 us
  Pallas kernels  32.4 us (58%)
  starting transfers between devices  12 us (21%)
  other arithmetic  4.53 us (8%)
  waiting for transfers between devices  2.77 us (5%)
  local copies, waits for them, and re-layouts  2.51 us (4%)
  between operations  0.76 us (1%)
    pallas_call x4, Pallas kernels, grads_call(): pl.pallas_call(kernel, grid_spec=grid_spec, out_shape=[dq_shape] + [dkv_s...  32.4 us
    ppermute x4, starting transfers between devices, shifted(): return lax.ppermute(block, axis, route)  12 us
    ppermute x4, waiting for transfers between devices, shifted(): return lax.ppermute(block, axis, route)  2.77 us
    another operation x3, other arithmetic  1.3 us
  transfers between devices with their start and end apart: 4, of which 1 were waited for; matrix products, arithmetic and copies ran while one was open for 5% of the time, Pallas kernels for 25%

profile of v5, /device:TPU:12, one launch (start us, length us, event | category | flops | bytes accessed | tf_op | source)
XLA Modules:
  0.0 55.0 jit_solution(2013711649465108909)
XLA Ops:
  0.6 1.0 %fusion.6 = (bf16[256,128]{1,0:T(8,128)(2,1)S(1)}, bf16[256,128]{1,0:T(8,128)(2,1)S(1)}, bf16[256,128]{1,0:T(8,128)(2,1)S(1)}, bf16[256,128]{1,0:T(8,128)(2,1)S(1)}) fusion(bf16[256,256]{1,0:T(8,128)(2,1)} %param.8, bf16[256,256]{1,0:T(8,128)(2,1)} %param.9), kind=kLoop, calls=%fused_computation.15 | loop fusion | bytes 524288 | tf_op jit(solution)/shard_map/slice | solution.py:266
  1.6 0.0 copy-start
  1.6 1.9 %collective-permute-start.1 = (bf16[256,512]{1,0:T(8,128)(2,1)S(1)}, bf16[256,512]{1,0:T(8,128)(2,1)S(1)}, u32[]{:S(2)}, u32[]{:S(2)}) collective-permute-start(bf16[256,512]{1,0:T(8,128)(2,1)S(1)} %pad_maximum_fusion.refs_5_), channel_id=1, source_target_pairs={{0,1},{1,2},{2,3},{3,4},{4,5},{5,6},{6,7},{7,8},{8,9},{9,10},{10,1... | collective-permute-start | bytes 786440 | tf_op jit(solution)/shard_map/ppermute | solution.py:20
  3.6 3.4 %collective-permute-start = (bf16[256,512]{1,0:T(8,128)(2,1)S(1)}, bf16[256,512]{1,0:T(8,128)(2,1)S(1)}, u32[]{:S(2)}, u32[]{:S(2)}) collective-permute-start(bf16[256,512]{1,0:T(8,128)(2,1)S(1)} %pad_maximum_fusion.refs_5_), channel_id=1, source_target_pairs={{0,2},{1,3},{2,4},{3,5},{4,6},{5,7},{6,8},{7,9},{8,10},{9,11},{10,... | collective-permute-start | bytes 786440 | tf_op jit(solution)/shard_map/ppermute | solution.py:20
  7.0 0.7 %copy.16 = s32[16,1]{1,0:T(8,128)S(1)} copy(s32[16,1]{0,1:T(1,128)} %bitcast.1) | data formatting | bytes 128 | tf_op jit(solution)/shard_map/reshape.26
  7.8 0.1 reduce
  7.9 0.1 convert_reduce_fusion
  8.0 0.8 %fusion.2.refs_4_ = f32[256,256]{1,0:T(8,128)} fusion(s32[256]{0:T(256)S(1)} %slice.33), kind=kLoop, calls=%fused_computation.7 | loop fusion | flops 262144 | bytes 263168 | tf_op jit(solution)/shard_map/jit(_where)/select_n | solution.py:259
  8.8 0.0 copy-done
  8.8 7.0 %shard_map.94 = (f32[256,2048]{1,0:T(8,128)}, f32[256,512]{1,0:T(8,128)}, f32[16,256]{1,0:T(8,128)}, bf16[4096,128]{1,0:T(8,128)(2,1)}, bf16[4096,128]{1,0:T(8,128)(2,1)}) custom-call(bf16[256,4096]{1,0:T(8,128)(2,1)} %refs_0_.3, bf16[256,4096]{1,0:T(8,128)(2,1)} %refs_1_.3, bf16[256,4096]{1,0:T(8,128)(2,1)} %refs_2_.3, f32[32,256]{1,0:T(8,128)} %refs_3_.7, ...), custom_call_target="tpu_custom_call" | custom-call | tf_op jit(solution)/shard_map/pallas_call | solution.py:231
  15.9 0.9 %compare_select_fusion.refs_4_ = f32[512,256]{1,0:T(8,128)} fusion(s32[256]{0:T(256)S(1)} %slice.33, s32[512]{0:T(512)S(1)} %slice.32), kind=kLoop, calls=%fused_computation.1 | loop fusion | flops 262144 | bytes 527360 | tf_op jit(solution)/shard_map/jit(_where)/select_n | solution.py:261
  16.8 0.0 collective-permute-done.1.refs_6_
  16.8 0.0 copy-start.1
  16.8 0.0 collective-permute-done.refs_5_
  16.8 0.0 copy-start.2
  16.8 0.7 %copy-done.1 = bf16[256,512]{1,0:T(8,128)(2,1)} copy-done((bf16[256,512]{1,0:T(8,128)(2,1)}, bf16[256,512]{1,0:T(8,128)(2,1)S(1)}, u32[]{:S(2)}) %copy-start.1) | copy-done | bytes 262168
  17.5 0.1 copy-done.2
  17.6 9.1 %shard_map.95 = (bf16[256,4096]{1,0:T(8,128)(2,1)}, bf16[256,512]{1,0:T(8,128)(2,1)}, bf16[256,512]{1,0:T(8,128)(2,1)}) custom-call(bf16[4096,128]{1,0:T(8,128)(2,1)} %get-tuple-element.19.refs_0_, bf16[4096,128]{1,0:T(8,128)(2,1)} %get-tuple-element.20.refs_1_, f32[16,256]{1,0:T(8,128)} %get-tuple-element.21.refs_2_, f32[32,256]{1,0:T(8,128)} %refs_3_.7, ...), custom_call_target="tpu_custom_call" | custom-call | tf_op jit(solution)/shard_map/pallas_call | solution.py:231
  26.7 9.9 %shard_map.96 = (f32[256,2048]{1,0:T(8,128)}, bf16[256,512]{1,0:T(8,128)(2,1)}, bf16[256,512]{1,0:T(8,128)(2,1)}, f32[16,256]{1,0:T(8,128)}, bf16[4096,128]{1,0:T(8,128)(2,1)}, /*index=5*/bf16[4096,128]{1,0:T(8,128)(2,1)}) custom-call(bf16[256,4096]{1,0:T(8,128)(2,1)} %refs_0_.3, ...), custom_call_target="tpu_custom_call", output_to_operand_aliasing={{1}: (7, {}), {2}: (8, {})} | custom-call | tf_op jit(solution)/shard_map/pallas_call | solution.py:231
  36.6 3.4 %collective-permute-start.2 = (bf16[256,512]{1,0:T(8,128)(2,1)}, bf16[256,512]{1,0:T(8,128)(2,1)S(1)}, u32[]{:S(2)}, u32[]{:S(2)}) collective-permute-start(bf16[256,512]{1,0:T(8,128)(2,1)} %get-tuple-element.33), channel_id=1, source_target_pairs={{1,0},{2,1},{3,2},{4,3},{5,4},{6,5},{7,6},{8,7},{9,8},{10,9},{11,1... | collective-permute-start | bytes 786440 | tf_op jit(solution)/shard_map/ppermute | solution.py:20
  39.9 3.3 %collective-permute-start.3 = (bf16[256,512]{1,0:T(8,128)(2,1)}, bf16[256,512]{1,0:T(8,128)(2,1)S(1)}, u32[]{:S(2)}, u32[]{:S(2)}) collective-permute-start(bf16[256,512]{1,0:T(8,128)(2,1)} %get-tuple-element.34), channel_id=1, source_target_pairs={{2,0},{3,1},{4,2},{5,3},{6,4},{7,5},{8,6},{9,7},{10,8},{11,9},{12,... | collective-permute-start | bytes 786440 | tf_op jit(solution)/shard_map/ppermute | solution.py:20
  43.2 6.5 %shard_map.97 = (bf16[256,4096]{1,0:T(8,128)(2,1)}, f32[256,512]{1,0:T(8,128)}) custom-call(bf16[4096,128]{1,0:T(8,128)(2,1)} %get-tuple-element.25.refs_0_, bf16[4096,128]{1,0:T(8,128)(2,1)} %get-tuple-element.26.refs_1_, f32[16,256]{1,0:T(8,128)} %get-tuple-element.27.refs_2_, f32[32,256]{1,0:T(8,128)} %refs_3_.7, ...), custom_call_target="tpu_custom_call", output_to_operand_aliasing={{0}: (7, {}), {1}: (8, {})} | custom-call | tf_op jit(solution)/shard_map/pallas_call | solution.py:231
  49.7 0.0 collective-permute-done.2
  49.7 2.8 %collective-permute-done.3 = bf16[256,512]{1,0:T(8,128)(2,1)S(1)} collective-permute-done((bf16[256,512]{1,0:T(8,128)(2,1)}, bf16[256,512]{1,0:T(8,128)(2,1)S(1)}, u32[]{:S(2)}, u32[]{:S(2)}) %collective-permute-start.3) | collective-permute-done | bytes 262176 | tf_op jit(solution)/shard_map/ppermute | solution.py:20
  52.5 1.1 %fusion.3 = (bf16[256,512]{1,0:T(8,128)(2,1)S(1)}, f32[256,512]{1,0:T(8,128)S(1)}) fusion(bf16[256,512]{1,0:T(8,128)(2,1)S(1)} %collective-permute-done.3, f32[256,512]{1,0:T(8,128)} %get-tuple-element.32, bf16[256,512]{1,0:T(8,128)(2,1)S(1)} %collective-permute-done.2), kind=kLoop, calls=%fused_computation.12 | loop fusion | flops 655360 | bytes 1835008 | tf_op jit(solution)/shard_map/convert.3
  53.7 0.7 %pad_maximum_fusion.1 = bf16[256,256]{1,0:T(8,128)(2,1)} fusion(bf16[256,128]{1,0:T(8,128)(2,1)S(1)} %get-tuple-element.40, bf16[256,128]{1,0:T(8,128)(2,1)S(1)} %get-tuple-element.39), kind=kLoop, calls=%fused_computation.8 | loop fusion | flops 262144 | bytes 262144 | tf_op jit(solution)/shard_map/concatenate | solution.py:282
  54.4 0.7 %fusion = bf16[256,256]{1,0:T(8,128)(2,1)} fusion(f32[256,128]{1,0:T(8,128)S(1)} %get-tuple-element.38, f32[256,128]{1,0:T(8,128)S(1)} %get-tuple-element.37), kind=kLoop, calls=%fused_computation.4 | loop fusion | flops 196608 | bytes 393216 | tf_op jit(solution)/shard_map/convert_element_type | solution.py:286
  (8 shorter events, 0.1 us)
Async XLA Ops:
  1.6 7.2 %copy-start = (bf16[256,512]{1,0:T(8,128)(2,1)}, bf16[256,512]{1,0:T(8,128)(2,1)S(1)}, u32[]{:S(2)}) copy-start(bf16[256,512]{1,0:T(8,128)(2,1)S(1)} %pad_maximum_fusion.refs_5_) | copy-start | bytes 786436
  1.6 15.2 %collective-permute-start.1 = (bf16[256,512]{1,0:T(8,128)(2,1)S(1)}, bf16[256,512]{1,0:T(8,128)(2,1)S(1)}, u32[]{:S(2)}, u32[]{:S(2)}) collective-permute-start(bf16[256,512]{1,0:T(8,128)(2,1)S(1)} %pad_maximum_fusion.refs_5_), channel_id=1, source_target_pairs={{0,1},{1,2},{2,3},{3,4},{4,5},{5,6},{6,7},{7,8},{8,9},{9,10},{10,1... | collective-permute-start | bytes 786440 | tf_op jit(solution)/shard_map/ppermute | solution.py:20
  3.6 13.2 %collective-permute-start = (bf16[256,512]{1,0:T(8,128)(2,1)S(1)}, bf16[256,512]{1,0:T(8,128)(2,1)S(1)}, u32[]{:S(2)}, u32[]{:S(2)}) collective-permute-start(bf16[256,512]{1,0:T(8,128)(2,1)S(1)} %pad_maximum_fusion.refs_5_), channel_id=1, source_target_pairs={{0,2},{1,3},{2,4},{3,5},{4,6},{5,7},{6,8},{7,9},{8,10},{9,11},{10,... | collective-permute-start | bytes 786440 | tf_op jit(solution)/shard_map/ppermute | solution.py:20
  16.8 0.7 %copy-start.1 = (bf16[256,512]{1,0:T(8,128)(2,1)}, bf16[256,512]{1,0:T(8,128)(2,1)S(1)}, u32[]{:S(2)}) copy-start(bf16[256,512]{1,0:T(8,128)(2,1)S(1)} %collective-permute-done.1.refs_6_) | copy-start | bytes 786436
  16.8 0.8 %copy-start.2 = (bf16[256,512]{1,0:T(8,128)(2,1)}, bf16[256,512]{1,0:T(8,128)(2,1)S(1)}, u32[]{:S(2)}) copy-start(bf16[256,512]{1,0:T(8,128)(2,1)S(1)} %collective-permute-done.refs_5_) | copy-start | bytes 786436
  36.6 13.2 %collective-permute-start.2 = (bf16[256,512]{1,0:T(8,128)(2,1)}, bf16[256,512]{1,0:T(8,128)(2,1)S(1)}, u32[]{:S(2)}, u32[]{:S(2)}) collective-permute-start(bf16[256,512]{1,0:T(8,128)(2,1)} %get-tuple-element.33), channel_id=1, source_target_pairs={{1,0},{2,1},{3,2},{4,3},{5,4},{6,5},{7,6},{8,7},{9,8},{10,9},{11,1... | collective-permute-start | bytes 786440 | tf_op jit(solution)/shard_map/ppermute | solution.py:20
  39.9 12.6 %collective-permute-start.3 = (bf16[256,512]{1,0:T(8,128)(2,1)}, bf16[256,512]{1,0:T(8,128)(2,1)S(1)}, u32[]{:S(2)}, u32[]{:S(2)}) collective-permute-start(bf16[256,512]{1,0:T(8,128)(2,1)} %get-tuple-element.34), channel_id=1, source_target_pairs={{2,0},{3,1},{4,2},{5,3},{6,4},{7,5},{8,6},{9,7},{10,8},{11,9},{12,... | collective-permute-start | bytes 786440 | tf_op jit(solution)/shard_map/ppermute | solution.py:20

commit v6 on v5

--- a/solution.py
+++ b/solution.py
@@ -10,7 +10,7 @@
 HD = 128
 MOST = 512
 KEY_TILE = 256
-HEADS_PER_STEP = 8
+HEADS_PER_STEP = 16
 NT_DIMS = (((1,), (1,)), ((), ()))
 
 

time: 55.9 us -> 54.9 us (0.982)
  Pallas kernels: 32.4 us -> 31.6 us
    pallas_call x4, Pallas kernels: 32.4 us -> 31.6 us  [grads_call(): pl.pallas_call(kernel, grid_spec=grid_spec, out_shape=[dq_shape] + [dkv_s...]
where the time goes in v6:
time: 54.9 us; the launch traced here: 54 us
  Pallas kernels  31.6 us (58%)
  starting transfers between devices  12 us (22%)
  other arithmetic  4.53 us (8%)
  waiting for transfers between devices  2.6 us (5%)
  local copies, waits for them, and re-layouts  2.51 us (5%)
  between operations  0.76 us (1%)
    pallas_call x4, Pallas kernels, grads_call(): pl.pallas_call(kernel, grid_spec=grid_spec, out_shape=[dq_shape] + [dkv_s...  31.6 us
    ppermute x4, starting transfers between devices, shifted(): return lax.ppermute(block, axis, route)  12 us
    ppermute x4, waiting for transfers between devices, shifted(): return lax.ppermute(block, axis, route)  2.6 us
    another operation x3, other arithmetic  1.3 us
  transfers between devices with their start and end apart: 4, of which 1 were waited for; matrix products, arithmetic and copies ran while one was open for 5% of the time, Pallas kernels for 25%

profile of v6, /device:TPU:12, one launch (start us, length us, event | category | flops | bytes accessed | tf_op | source)
XLA Modules:
  0.0 54.0 jit_solution(9101404313399496453)
XLA Ops:
  0.6 1.0 %fusion.6 = (bf16[256,128]{1,0:T(8,128)(2,1)S(1)}, bf16[256,128]{1,0:T(8,128)(2,1)S(1)}, bf16[256,128]{1,0:T(8,128)(2,1)S(1)}, bf16[256,128]{1,0:T(8,128)(2,1)S(1)}) fusion(bf16[256,256]{1,0:T(8,128)(2,1)} %param.8, bf16[256,256]{1,0:T(8,128)(2,1)} %param.9), kind=kLoop, calls=%fused_computation.15 | loop fusion | bytes 524288 | tf_op jit(solution)/shard_map/slice | solution.py:266
  1.6 0.0 copy-start
  1.6 1.9 %collective-permute-start.1 = (bf16[256,512]{1,0:T(8,128)(2,1)S(1)}, bf16[256,512]{1,0:T(8,128)(2,1)S(1)}, u32[]{:S(2)}, u32[]{:S(2)}) collective-permute-start(bf16[256,512]{1,0:T(8,128)(2,1)S(1)} %pad_maximum_fusion.refs_5_), channel_id=1, source_target_pairs={{0,1},{1,2},{2,3},{3,4},{4,5},{5,6},{6,7},{7,8},{8,9},{9,10},{10,1... | collective-permute-start | bytes 786440 | tf_op jit(solution)/shard_map/ppermute | solution.py:20
  3.6 3.4 %collective-permute-start = (bf16[256,512]{1,0:T(8,128)(2,1)S(1)}, bf16[256,512]{1,0:T(8,128)(2,1)S(1)}, u32[]{:S(2)}, u32[]{:S(2)}) collective-permute-start(bf16[256,512]{1,0:T(8,128)(2,1)S(1)} %pad_maximum_fusion.refs_5_), channel_id=1, source_target_pairs={{0,2},{1,3},{2,4},{3,5},{4,6},{5,7},{6,8},{7,9},{8,10},{9,11},{10,... | collective-permute-start | bytes 786440 | tf_op jit(solution)/shard_map/ppermute | solution.py:20
  7.0 0.7 %copy.16 = s32[16,1]{1,0:T(8,128)S(1)} copy(s32[16,1]{0,1:T(1,128)} %bitcast.1) | data formatting | bytes 128 | tf_op jit(solution)/shard_map/reshape.26
  7.8 0.1 reduce
  7.9 0.1 convert_reduce_fusion
  8.0 0.8 %fusion.2.refs_4_ = f32[256,256]{1,0:T(8,128)} fusion(s32[256]{0:T(256)S(1)} %slice.33), kind=kLoop, calls=%fused_computation.7 | loop fusion | flops 262144 | bytes 263168 | tf_op jit(solution)/shard_map/jit(_where)/select_n | solution.py:259
  8.8 0.0 copy-done
  8.8 7.0 %shard_map.94 = (f32[256,2048]{1,0:T(8,128)}, f32[256,512]{1,0:T(8,128)}, f32[16,256]{1,0:T(8,128)}, bf16[4096,128]{1,0:T(8,128)(2,1)}, bf16[4096,128]{1,0:T(8,128)(2,1)}) custom-call(bf16[256,4096]{1,0:T(8,128)(2,1)} %refs_0_.3, bf16[256,4096]{1,0:T(8,128)(2,1)} %refs_1_.3, bf16[256,4096]{1,0:T(8,128)(2,1)} %refs_2_.3, f32[32,256]{1,0:T(8,128)} %refs_3_.7, ...), custom_call_target="tpu_custom_call" | custom-call | tf_op jit(solution)/shard_map/pallas_call | solution.py:231
  15.8 0.9 %compare_select_fusion.refs_4_ = f32[512,256]{1,0:T(8,128)} fusion(s32[256]{0:T(256)S(1)} %slice.33, s32[512]{0:T(512)S(1)} %slice.32), kind=kLoop, calls=%fused_computation.1 | loop fusion | flops 262144 | bytes 527360 | tf_op jit(solution)/shard_map/jit(_where)/select_n | solution.py:261
  16.8 0.0 collective-permute-done.1.refs_6_
  16.8 0.0 copy-start.1
  16.8 0.0 collective-permute-done.refs_5_
  16.8 0.0 copy-start.2
  16.8 0.7 %copy-done.1 = bf16[256,512]{1,0:T(8,128)(2,1)} copy-done((bf16[256,512]{1,0:T(8,128)(2,1)}, bf16[256,512]{1,0:T(8,128)(2,1)S(1)}, u32[]{:S(2)}) %copy-start.1) | copy-done | bytes 262168
  17.5 0.1 copy-done.2
  17.6 8.6 %shard_map.95 = (bf16[256,4096]{1,0:T(8,128)(2,1)}, bf16[256,512]{1,0:T(8,128)(2,1)}, bf16[256,512]{1,0:T(8,128)(2,1)}) custom-call(bf16[4096,128]{1,0:T(8,128)(2,1)} %get-tuple-element.19.refs_0_, bf16[4096,128]{1,0:T(8,128)(2,1)} %get-tuple-element.20.refs_1_, f32[16,256]{1,0:T(8,128)} %get-tuple-element.21.refs_2_, f32[32,256]{1,0:T(8,128)} %refs_3_.7, ...), custom_call_target="tpu_custom_call" | custom-call | tf_op jit(solution)/shard_map/pallas_call | solution.py:231
  26.2 9.3 %shard_map.96 = (f32[256,2048]{1,0:T(8,128)}, bf16[256,512]{1,0:T(8,128)(2,1)}, bf16[256,512]{1,0:T(8,128)(2,1)}, f32[16,256]{1,0:T(8,128)}, bf16[4096,128]{1,0:T(8,128)(2,1)}, /*index=5*/bf16[4096,128]{1,0:T(8,128)(2,1)}) custom-call(bf16[256,4096]{1,0:T(8,128)(2,1)} %refs_0_.3, ...), custom_call_target="tpu_custom_call", output_to_operand_aliasing={{1}: (7, {}), {2}: (8, {})} | custom-call | tf_op jit(solution)/shard_map/pallas_call | solution.py:231
  35.5 3.4 %collective-permute-start.2 = (bf16[256,512]{1,0:T(8,128)(2,1)}, bf16[256,512]{1,0:T(8,128)(2,1)S(1)}, u32[]{:S(2)}, u32[]{:S(2)}) collective-permute-start(bf16[256,512]{1,0:T(8,128)(2,1)} %get-tuple-element.33), channel_id=1, source_target_pairs={{1,0},{2,1},{3,2},{4,3},{5,4},{6,5},{7,6},{8,7},{9,8},{10,9},{11,1... | collective-permute-start | bytes 786440 | tf_op jit(solution)/shard_map/ppermute | solution.py:20
  38.9 3.3 %collective-permute-start.3 = (bf16[256,512]{1,0:T(8,128)(2,1)}, bf16[256,512]{1,0:T(8,128)(2,1)S(1)}, u32[]{:S(2)}, u32[]{:S(2)}) collective-permute-start(bf16[256,512]{1,0:T(8,128)(2,1)} %get-tuple-element.34), channel_id=1, source_target_pairs={{2,0},{3,1},{4,2},{5,3},{6,4},{7,5},{8,6},{9,7},{10,8},{11,9},{12,... | collective-permute-start | bytes 786440 | tf_op jit(solution)/shard_map/ppermute | solution.py:20
  42.2 6.7 %shard_map.97 = (bf16[256,4096]{1,0:T(8,128)(2,1)}, f32[256,512]{1,0:T(8,128)}) custom-call(bf16[4096,128]{1,0:T(8,128)(2,1)} %get-tuple-element.25.refs_0_, bf16[4096,128]{1,0:T(8,128)(2,1)} %get-tuple-element.26.refs_1_, f32[16,256]{1,0:T(8,128)} %get-tuple-element.27.refs_2_, f32[32,256]{1,0:T(8,128)} %refs_3_.7, ...), custom_call_target="tpu_custom_call", output_to_operand_aliasing={{0}: (7, {}), {1}: (8, {})} | custom-call | tf_op jit(solution)/shard_map/pallas_call | solution.py:231
  48.9 0.0 collective-permute-done.2
  48.9 2.6 %collective-permute-done.3 = bf16[256,512]{1,0:T(8,128)(2,1)S(1)} collective-permute-done((bf16[256,512]{1,0:T(8,128)(2,1)}, bf16[256,512]{1,0:T(8,128)(2,1)S(1)}, u32[]{:S(2)}, u32[]{:S(2)}) %collective-permute-start.3) | collective-permute-done | bytes 262176 | tf_op jit(solution)/shard_map/ppermute | solution.py:20
  51.5 1.1 %fusion.3 = (bf16[256,512]{1,0:T(8,128)(2,1)S(1)}, f32[256,512]{1,0:T(8,128)S(1)}) fusion(bf16[256,512]{1,0:T(8,128)(2,1)S(1)} %collective-permute-done.3, f32[256,512]{1,0:T(8,128)} %get-tuple-element.32, bf16[256,512]{1,0:T(8,128)(2,1)S(1)} %collective-permute-done.2), kind=kLoop, calls=%fused_computation.12 | loop fusion | flops 655360 | bytes 1835008 | tf_op jit(solution)/shard_map/convert.3
  52.7 0.7 %pad_maximum_fusion.1 = bf16[256,256]{1,0:T(8,128)(2,1)} fusion(bf16[256,128]{1,0:T(8,128)(2,1)S(1)} %get-tuple-element.40, bf16[256,128]{1,0:T(8,128)(2,1)S(1)} %get-tuple-element.39), kind=kLoop, calls=%fused_computation.8 | loop fusion | flops 262144 | bytes 262144 | tf_op jit(solution)/shard_map/concatenate | solution.py:282
  53.3 0.7 %fusion = bf16[256,256]{1,0:T(8,128)(2,1)} fusion(f32[256,128]{1,0:T(8,128)S(1)} %get-tuple-element.38, f32[256,128]{1,0:T(8,128)S(1)} %get-tuple-element.37), kind=kLoop, calls=%fused_computation.4 | loop fusion | flops 196608 | bytes 393216 | tf_op jit(solution)/shard_map/convert_element_type | solution.py:286
  (8 shorter events, 0.1 us)
Async XLA Ops:
  1.6 7.2 %copy-start = (bf16[256,512]{1,0:T(8,128)(2,1)}, bf16[256,512]{1,0:T(8,128)(2,1)S(1)}, u32[]{:S(2)}) copy-start(bf16[256,512]{1,0:T(8,128)(2,1)S(1)} %pad_maximum_fusion.refs_5_) | copy-start | bytes 786436
  1.6 15.1 %collective-permute-start.1 = (bf16[256,512]{1,0:T(8,128)(2,1)S(1)}, bf16[256,512]{1,0:T(8,128)(2,1)S(1)}, u32[]{:S(2)}, u32[]{:S(2)}) collective-permute-start(bf16[256,512]{1,0:T(8,128)(2,1)S(1)} %pad_maximum_fusion.refs_5_), channel_id=1, source_target_pairs={{0,1},{1,2},{2,3},{3,4},{4,5},{5,6},{6,7},{7,8},{8,9},{9,10},{10,1... | collective-permute-start | bytes 786440 | tf_op jit(solution)/shard_map/ppermute | solution.py:20
  3.6 13.2 %collective-permute-start = (bf16[256,512]{1,0:T(8,128)(2,1)S(1)}, bf16[256,512]{1,0:T(8,128)(2,1)S(1)}, u32[]{:S(2)}, u32[]{:S(2)}) collective-permute-start(bf16[256,512]{1,0:T(8,128)(2,1)S(1)} %pad_maximum_fusion.refs_5_), channel_id=1, source_target_pairs={{0,2},{1,3},{2,4},{3,5},{4,6},{5,7},{6,8},{7,9},{8,10},{9,11},{10,... | collective-permute-start | bytes 786440 | tf_op jit(solution)/shard_map/ppermute | solution.py:20
  16.8 0.7 %copy-start.1 = (bf16[256,512]{1,0:T(8,128)(2,1)}, bf16[256,512]{1,0:T(8,128)(2,1)S(1)}, u32[]{:S(2)}) copy-start(bf16[256,512]{1,0:T(8,128)(2,1)S(1)} %collective-permute-done.1.refs_6_) | copy-start | bytes 786436
  16.8 0.8 %copy-start.2 = (bf16[256,512]{1,0:T(8,128)(2,1)}, bf16[256,512]{1,0:T(8,128)(2,1)S(1)}, u32[]{:S(2)}) copy-start(bf16[256,512]{1,0:T(8,128)(2,1)S(1)} %collective-permute-done.refs_5_) | copy-start | bytes 786436
  35.5 13.3 %collective-permute-start.2 = (bf16[256,512]{1,0:T(8,128)(2,1)}, bf16[256,512]{1,0:T(8,128)(2,1)S(1)}, u32[]{:S(2)}, u32[]{:S(2)}) collective-permute-start(bf16[256,512]{1,0:T(8,128)(2,1)} %get-tuple-element.33), channel_id=1, source_target_pairs={{1,0},{2,1},{3,2},{4,3},{5,4},{6,5},{7,6},{8,7},{9,8},{10,9},{11,1... | collective-permute-start | bytes 786440 | tf_op jit(solution)/shard_map/ppermute | solution.py:20
  38.9 12.6 %collective-permute-start.3 = (bf16[256,512]{1,0:T(8,128)(2,1)}, bf16[256,512]{1,0:T(8,128)(2,1)S(1)}, u32[]{:S(2)}, u32[]{:S(2)}) collective-permute-start(bf16[256,512]{1,0:T(8,128)(2,1)} %get-tuple-element.34), channel_id=1, source_target_pairs={{2,0},{3,1},{4,2},{5,3},{6,4},{7,5},{8,6},{9,7},{10,8},{11,9},{12,... | collective-permute-start | bytes 786440 | tf_op jit(solution)/shard_map/ppermute | solution.py:20

commit v7 on v6

--- a/solution.py
+++ b/solution.py
@@ -11,6 +11,7 @@
 MOST = 512
 KEY_TILE = 256
 HEADS_PER_STEP = 16
+OWN_HEADS_PER_STEP = 8
 NT_DIMS = (((1,), (1,)), ((), ()))
 
 
@@ -21,7 +22,7 @@
 
 
 def make_kernel(tok, reach, remote, dq_in, dq_final, n_alias, delta_in):
-    hb = HEADS_PER_STEP
+    hb = HEADS_PER_STEP if remote else OWN_HEADS_PER_STEP
     pieces = list(range(reach)) if remote else [reach]
     tiles_per_piece = tok // KEY_TILE
     n_rows = len(pieces) * tok
@@ -139,7 +140,7 @@
     n_heads = width // HD
     kvh = kv_pieces[0].shape[1] // (2 * HD)
     heads_per_group = n_heads // kvh
-    hb = HEADS_PER_STEP
+    hb = HEADS_PER_STEP if remote else OWN_HEADS_PER_STEP
     nb = heads_per_group // hb
     dq_final = dq_part is not None
     pieces = list(range(reach)) if remote else [reach]

time: 54.9 us -> 54.7 us (level)
  no operation moved by 1% of the time
where the time goes in v7:
time: 54.7 us; the launch traced here: 53.8 us
  Pallas kernels  31.3 us (57%)
  starting transfers between devices  12 us (22%)
  other arithmetic  4.53 us (8%)
  waiting for transfers between devices  2.78 us (5%)
  local copies, waits for them, and re-layouts  2.51 us (5%)
  between operations  0.76 us (1%)
    pallas_call x4, Pallas kernels, grads_call(): pl.pallas_call(kernel, grid_spec=grid_spec, out_shape=[dq_shape] + [dkv_s...  31.3 us
    ppermute x4, starting transfers between devices, shifted(): return lax.ppermute(block, axis, route)  12 us
    ppermute x4, waiting for transfers between devices, shifted(): return lax.ppermute(block, axis, route)  2.78 us
    another operation x3, other arithmetic  1.3 us
  transfers between devices with their start and end apart: 4, of which 1 were waited for; matrix products, arithmetic and copies ran while one was open for 5% of the time, Pallas kernels for 25%

profile of v7, /device:TPU:12, one launch (start us, length us, event | category | flops | bytes accessed | tf_op | source)
XLA Modules:
  0.0 53.8 jit_solution(14132767830339510719)
XLA Ops:
  0.6 1.0 %fusion.6 = (bf16[256,128]{1,0:T(8,128)(2,1)S(1)}, bf16[256,128]{1,0:T(8,128)(2,1)S(1)}, bf16[256,128]{1,0:T(8,128)(2,1)S(1)}, bf16[256,128]{1,0:T(8,128)(2,1)S(1)}) fusion(bf16[256,256]{1,0:T(8,128)(2,1)} %param.8, bf16[256,256]{1,0:T(8,128)(2,1)} %param.9), kind=kLoop, calls=%fused_computation.15 | loop fusion | bytes 524288 | tf_op jit(solution)/shard_map/slice | solution.py:267
  1.6 0.0 copy-start
  1.6 1.9 %collective-permute-start.1 = (bf16[256,512]{1,0:T(8,128)(2,1)S(1)}, bf16[256,512]{1,0:T(8,128)(2,1)S(1)}, u32[]{:S(2)}, u32[]{:S(2)}) collective-permute-start(bf16[256,512]{1,0:T(8,128)(2,1)S(1)} %pad_maximum_fusion.refs_5_), channel_id=1, source_target_pairs={{0,1},{1,2},{2,3},{3,4},{4,5},{5,6},{6,7},{7,8},{8,9},{9,10},{10,1... | collective-permute-start | bytes 786440 | tf_op jit(solution)/shard_map/ppermute | solution.py:21
  3.6 3.4 %collective-permute-start = (bf16[256,512]{1,0:T(8,128)(2,1)S(1)}, bf16[256,512]{1,0:T(8,128)(2,1)S(1)}, u32[]{:S(2)}, u32[]{:S(2)}) collective-permute-start(bf16[256,512]{1,0:T(8,128)(2,1)S(1)} %pad_maximum_fusion.refs_5_), channel_id=1, source_target_pairs={{0,2},{1,3},{2,4},{3,5},{4,6},{5,7},{6,8},{7,9},{8,10},{9,11},{10,... | collective-permute-start | bytes 786440 | tf_op jit(solution)/shard_map/ppermute | solution.py:21
  7.0 0.7 %copy.16 = s32[16,1]{1,0:T(8,128)S(1)} copy(s32[16,1]{0,1:T(1,128)} %bitcast.1) | data formatting | bytes 128 | tf_op jit(solution)/shard_map/reshape.26
  7.8 0.1 reduce
  7.9 0.1 convert_reduce_fusion
  8.0 0.8 %fusion.2.refs_4_ = f32[256,256]{1,0:T(8,128)} fusion(s32[256]{0:T(256)S(1)} %slice.33), kind=kLoop, calls=%fused_computation.7 | loop fusion | flops 262144 | bytes 263168 | tf_op jit(solution)/shard_map/jit(_where)/select_n | solution.py:260
  8.8 0.0 copy-done
  8.8 7.0 %shard_map.94 = (f32[256,2048]{1,0:T(8,128)}, f32[256,512]{1,0:T(8,128)}, f32[16,256]{1,0:T(8,128)}, bf16[4096,128]{1,0:T(8,128)(2,1)}, bf16[4096,128]{1,0:T(8,128)(2,1)}) custom-call(bf16[256,4096]{1,0:T(8,128)(2,1)} %refs_0_.3, bf16[256,4096]{1,0:T(8,128)(2,1)} %refs_1_.3, bf16[256,4096]{1,0:T(8,128)(2,1)} %refs_2_.3, f32[32,256]{1,0:T(8,128)} %refs_3_.7, ...), custom_call_target="tpu_custom_call" | custom-call | tf_op jit(solution)/shard_map/pallas_call | solution.py:232
  15.9 0.9 %compare_select_fusion.refs_4_ = f32[512,256]{1,0:T(8,128)} fusion(s32[256]{0:T(256)S(1)} %slice.33, s32[512]{0:T(512)S(1)} %slice.32), kind=kLoop, calls=%fused_computation.1 | loop fusion | flops 262144 | bytes 527360 | tf_op jit(solution)/shard_map/jit(_where)/select_n | solution.py:262
  16.8 0.0 collective-permute-done.1.refs_6_
  16.8 0.0 copy-start.1
  16.8 0.0 collective-permute-done.refs_5_
  16.8 0.0 copy-start.2
  16.8 0.7 %copy-done.1 = bf16[256,512]{1,0:T(8,128)(2,1)} copy-done((bf16[256,512]{1,0:T(8,128)(2,1)}, bf16[256,512]{1,0:T(8,128)(2,1)S(1)}, u32[]{:S(2)}) %copy-start.1) | copy-done | bytes 262168
  17.5 0.1 copy-done.2
  17.6 8.6 %shard_map.95 = (bf16[256,4096]{1,0:T(8,128)(2,1)}, bf16[256,512]{1,0:T(8,128)(2,1)}, bf16[256,512]{1,0:T(8,128)(2,1)}) custom-call(bf16[4096,128]{1,0:T(8,128)(2,1)} %get-tuple-element.19.refs_0_, bf16[4096,128]{1,0:T(8,128)(2,1)} %get-tuple-element.20.refs_1_, f32[16,256]{1,0:T(8,128)} %get-tuple-element.21.refs_2_, f32[32,256]{1,0:T(8,128)} %refs_3_.7, ...), custom_call_target="tpu_custom_call" | custom-call | tf_op jit(solution)/shard_map/pallas_call | solution.py:232
  26.2 9.1 %shard_map.96 = (f32[256,2048]{1,0:T(8,128)}, bf16[256,512]{1,0:T(8,128)(2,1)}, bf16[256,512]{1,0:T(8,128)(2,1)}, f32[16,256]{1,0:T(8,128)}, bf16[4096,128]{1,0:T(8,128)(2,1)}, /*index=5*/bf16[4096,128]{1,0:T(8,128)(2,1)}) custom-call(bf16[256,4096]{1,0:T(8,128)(2,1)} %refs_0_.3, ...), custom_call_target="tpu_custom_call", output_to_operand_aliasing={{1}: (7, {}), {2}: (8, {})} | custom-call | tf_op jit(solution)/shard_map/pallas_call | solution.py:232
  35.4 3.4 %collective-permute-start.2 = (bf16[256,512]{1,0:T(8,128)(2,1)}, bf16[256,512]{1,0:T(8,128)(2,1)S(1)}, u32[]{:S(2)}, u32[]{:S(2)}) collective-permute-start(bf16[256,512]{1,0:T(8,128)(2,1)} %get-tuple-element.33), channel_id=1, source_target_pairs={{1,0},{2,1},{3,2},{4,3},{5,4},{6,5},{7,6},{8,7},{9,8},{10,9},{11,1... | collective-permute-start | bytes 786440 | tf_op jit(solution)/shard_map/ppermute | solution.py:21
  38.7 3.3 %collective-permute-start.3 = (bf16[256,512]{1,0:T(8,128)(2,1)}, bf16[256,512]{1,0:T(8,128)(2,1)S(1)}, u32[]{:S(2)}, u32[]{:S(2)}) collective-permute-start(bf16[256,512]{1,0:T(8,128)(2,1)} %get-tuple-element.34), channel_id=1, source_target_pairs={{2,0},{3,1},{4,2},{5,3},{6,4},{7,5},{8,6},{9,7},{10,8},{11,9},{12,... | collective-permute-start | bytes 786440 | tf_op jit(solution)/shard_map/ppermute | solution.py:21
  42.0 6.5 %shard_map.97 = (bf16[256,4096]{1,0:T(8,128)(2,1)}, f32[256,512]{1,0:T(8,128)}) custom-call(bf16[4096,128]{1,0:T(8,128)(2,1)} %get-tuple-element.25.refs_0_, bf16[4096,128]{1,0:T(8,128)(2,1)} %get-tuple-element.26.refs_1_, f32[16,256]{1,0:T(8,128)} %get-tuple-element.27.refs_2_, f32[32,256]{1,0:T(8,128)} %refs_3_.7, ...), custom_call_target="tpu_custom_call", output_to_operand_aliasing={{0}: (7, {}), {1}: (8, {})} | custom-call | tf_op jit(solution)/shard_map/pallas_call | solution.py:232
  48.5 0.0 collective-permute-done.2
  48.5 2.8 %collective-permute-done.3 = bf16[256,512]{1,0:T(8,128)(2,1)S(1)} collective-permute-done((bf16[256,512]{1,0:T(8,128)(2,1)}, bf16[256,512]{1,0:T(8,128)(2,1)S(1)}, u32[]{:S(2)}, u32[]{:S(2)}) %collective-permute-start.3) | collective-permute-done | bytes 262176 | tf_op jit(solution)/shard_map/ppermute | solution.py:21
  51.3 1.1 %fusion.3 = (bf16[256,512]{1,0:T(8,128)(2,1)S(1)}, f32[256,512]{1,0:T(8,128)S(1)}) fusion(bf16[256,512]{1,0:T(8,128)(2,1)S(1)} %collective-permute-done.3, f32[256,512]{1,0:T(8,128)} %get-tuple-element.32, bf16[256,512]{1,0:T(8,128)(2,1)S(1)} %collective-permute-done.2), kind=kLoop, calls=%fused_computation.12 | loop fusion | flops 655360 | bytes 1835008 | tf_op jit(solution)/shard_map/convert.3
  52.5 0.7 %pad_maximum_fusion.1 = bf16[256,256]{1,0:T(8,128)(2,1)} fusion(bf16[256,128]{1,0:T(8,128)(2,1)S(1)} %get-tuple-element.40, bf16[256,128]{1,0:T(8,128)(2,1)S(1)} %get-tuple-element.39), kind=kLoop, calls=%fused_computation.8 | loop fusion | flops 262144 | bytes 262144 | tf_op jit(solution)/shard_map/concatenate | solution.py:283
  53.2 0.7 %fusion = bf16[256,256]{1,0:T(8,128)(2,1)} fusion(f32[256,128]{1,0:T(8,128)S(1)} %get-tuple-element.38, f32[256,128]{1,0:T(8,128)S(1)} %get-tuple-element.37), kind=kLoop, calls=%fused_computation.4 | loop fusion | flops 196608 | bytes 393216 | tf_op jit(solution)/shard_map/convert_element_type | solution.py:287
  (8 shorter events, 0.1 us)
Async XLA Ops:
  1.6 7.2 %copy-start = (bf16[256,512]{1,0:T(8,128)(2,1)}, bf16[256,512]{1,0:T(8,128)(2,1)S(1)}, u32[]{:S(2)}) copy-start(bf16[256,512]{1,0:T(8,128)(2,1)S(1)} %pad_maximum_fusion.refs_5_) | copy-start | bytes 786436
  1.6 15.2 %collective-permute-start.1 = (bf16[256,512]{1,0:T(8,128)(2,1)S(1)}, bf16[256,512]{1,0:T(8,128)(2,1)S(1)}, u32[]{:S(2)}, u32[]{:S(2)}) collective-permute-start(bf16[256,512]{1,0:T(8,128)(2,1)S(1)} %pad_maximum_fusion.refs_5_), channel_id=1, source_target_pairs={{0,1},{1,2},{2,3},{3,4},{4,5},{5,6},{6,7},{7,8},{8,9},{9,10},{10,1... | collective-permute-start | bytes 786440 | tf_op jit(solution)/shard_map/ppermute | solution.py:21
  3.6 13.2 %collective-permute-start = (bf16[256,512]{1,0:T(8,128)(2,1)S(1)}, bf16[256,512]{1,0:T(8,128)(2,1)S(1)}, u32[]{:S(2)}, u32[]{:S(2)}) collective-permute-start(bf16[256,512]{1,0:T(8,128)(2,1)S(1)} %pad_maximum_fusion.refs_5_), channel_id=1, source_target_pairs={{0,2},{1,3},{2,4},{3,5},{4,6},{5,7},{6,8},{7,9},{8,10},{9,11},{10,... | collective-permute-start | bytes 786440 | tf_op jit(solution)/shard_map/ppermute | solution.py:21
  16.8 0.7 %copy-start.1 = (bf16[256,512]{1,0:T(8,128)(2,1)}, bf16[256,512]{1,0:T(8,128)(2,1)S(1)}, u32[]{:S(2)}) copy-start(bf16[256,512]{1,0:T(8,128)(2,1)S(1)} %collective-permute-done.1.refs_6_) | copy-start | bytes 786436
  16.8 0.8 %copy-start.2 = (bf16[256,512]{1,0:T(8,128)(2,1)}, bf16[256,512]{1,0:T(8,128)(2,1)S(1)}, u32[]{:S(2)}) copy-start(bf16[256,512]{1,0:T(8,128)(2,1)S(1)} %collective-permute-done.refs_5_) | copy-start | bytes 786436
  35.4 13.2 %collective-permute-start.2 = (bf16[256,512]{1,0:T(8,128)(2,1)}, bf16[256,512]{1,0:T(8,128)(2,1)S(1)}, u32[]{:S(2)}, u32[]{:S(2)}) collective-permute-start(bf16[256,512]{1,0:T(8,128)(2,1)} %get-tuple-element.33), channel_id=1, source_target_pairs={{1,0},{2,1},{3,2},{4,3},{5,4},{6,5},{7,6},{8,7},{9,8},{10,9},{11,1... | collective-permute-start | bytes 786440 | tf_op jit(solution)/shard_map/ppermute | solution.py:21
  38.7 12.6 %collective-permute-start.3 = (bf16[256,512]{1,0:T(8,128)(2,1)}, bf16[256,512]{1,0:T(8,128)(2,1)S(1)}, u32[]{:S(2)}, u32[]{:S(2)}) collective-permute-start(bf16[256,512]{1,0:T(8,128)(2,1)} %get-tuple-element.34), channel_id=1, source_target_pairs={{2,0},{3,1},{4,2},{5,3},{6,4},{7,5},{8,6},{9,7},{10,8},{11,9},{12,... | collective-permute-start | bytes 786440 | tf_op jit(solution)/shard_map/ppermute | solution.py:21
